TPU v7x, 128 devices: a whole 4x4x4 slice. The times are simulated.
128 devices in a mesh: seq: 16 (over x_hi, z, core), tensor: 8 (over y, x_lo).
Axes of the slice: x: 4 (x_hi: 2, x_lo: 2; x = x_hi * 2 + x_lo), y: 4, z: 4, core: 2. Of those that a mesh axis runs over, the one named last changes fastest.
Arguments:
- layer_input: bfloat16 [16384, 1024], P('seq'), may hold values from -3 to 3
- queries: bfloat16 [16384, 1024], P('seq', 'tensor'), may hold values from -2.5 to 2.5
- fresh_keys: bfloat16 [16384, 1024], P('seq', 'tensor'), may hold values from -3 to 3
- fresh_values: bfloat16 [16384, 1024], P('seq', 'tensor'), may hold values from -6 to 6
- cached_keys: bfloat16 [12288, 1024], P('seq', 'tensor'), may hold values from -2.5 to 2.5
- cached_values: bfloat16 [12288, 1024], P('seq', 'tensor'), may hold values from -6 to 6
- start_position: int32 [1], replicated, may hold values from 12288 to 12383
- bias_table: float32 [32, 16], P(None, 'tensor'), may hold values from -4 to 4
- out_weight: bfloat16 [1024, 1024], P('tensor'), may hold values from -0.1875 to 0.1875
- norm_gain: float32 [1024], replicated, may hold values from 0.1 to 1.9
- routes: int32 [16384, 2], P('seq'), may hold values from 0 to 7, all different within a row; in each aligned block of 1024 rows (0 to 1023, 1024 to 2047, ...) at most 384 rows name the same one
- route_weights: float32 [16384, 2], P('seq'), may hold values from 0.2 to 1
- expert_in: bfloat16 [8, 1024, 2, 2816], P(None, None, None, 'tensor'), may hold values from -0.1875 to 0.1875
- expert_out: bfloat16 [8, 2816, 1024], P(None, 'tensor'), may hold values from -0.109375 to 0.109375
Outputs:
- mixed: bfloat16 [16384, 1024], P('seq', 'tensor')
Inputs may be any that keep to these rules, and one draw needn't show every extreme that they name: `routes`: in the rows of one device (aligned blocks of 1024 rows) no expert is named more than 384 times; some expert reaches 384 in every draw. A row names 2 different experts.
All inputs are finite; a program needn't handle non-finite values.
Results may differ from a plain program's by a relative error of at most 0.019.
Values may be sent and summed in bfloat16 or wider, within the bound.
No kernel may reach another device: no remote copies, remote signals or barrier semaphores. Data moves between devices by JAX's collectives and lax.ppermute only.
A program may use at most 192 MiB of HBM per device.

v0:
```python
import math

import jax
import jax.numpy as jnp
from jax import lax
from jax.experimental import pallas as pl
from jax.experimental.pallas import tpu as pltpu
from jax.sharding import PartitionSpec as P

D = 1024
HEAD_DIM = 64
TOP = 2
CAP = 384
KEY_TILE = 512
ROW_BLOCK = 128


bucket_edges = [edge for edge in range(1, 17)] + [
    math.ceil(16 * 8 ** (level / 16)) for level in range(1, 16)
]
far_edge = bucket_edges[-1]
epsilon = 1e-06
lowest = -1e30


def attn_kernel(scal_ref, dtab_ref, q_ref, k_ref, v_ref, m_in, l_in, acc_in, m_ref, l_ref, acc_ref):
    t = pl.program_id(0)
    tk = k_ref.shape[0]
    rows_all = q_ref.shape[0]

    @pl.when(t == 0)
    def _():
        m_ref[...] = m_in[...]
        l_ref[...] = l_in[...]
        acc_ref[...] = acc_in[...]

    n_valid = scal_ref[2]
    active = (t < n_valid) & ((t < scal_ref[3]) | (t >= scal_ref[4]))
    half_blocks = rows_all // ROW_BLOCK // 2

    def update(r, near, qk_off):
        rows = pl.ds(r * ROW_BLOCK, ROW_BLOCK)
        q = q_ref[rows, :]
        k = k_ref[...]
        v = v_ref[...]
        lane = lax.broadcasted_iota(jnp.int32, (1, q.shape[1]), 1) < HEAD_DIM
        zero_q = jnp.zeros_like(q)
        if near:
            base = qk_off + r * ROW_BLOCK - t * tk
            d = (
                base
                + lax.broadcasted_iota(jnp.int32, (ROW_BLOCK, tk), 0)
                - lax.broadcasted_iota(jnp.int32, (ROW_BLOCK, tk), 1)
            )
            allowed = d >= 0
            bucket = jnp.zeros(d.shape, jnp.int32)
            for edge in bucket_edges:
                bucket = bucket + (d >= edge).astype(jnp.int32)
        news = []
        alphas = []
        pvs = []
        for h in range(2):
            qh = jnp.where(lane, q, zero_q) if h == 0 else jnp.where(lane, zero_q, q)
            s = lax.dot_general(
                qh, k, (((1,), (1,)), ((), ())), preferred_element_type=jnp.float32
            )
            if near:
                delta = jnp.zeros(s.shape, jnp.float32)
                for level in range(len(bucket_edges)):
                    delta = jnp.where(bucket == level, dtab_ref[level, h], delta)
                s = jnp.where(allowed, s + delta, -jnp.inf)
            m_prev = m_ref[h, rows, :]
            m_curr = jnp.max(s, axis=1, keepdims=True)
            m_next = jnp.maximum(m_prev, m_curr)
            p = jnp.exp(s - jnp.tile(m_next, (1, tk // m_next.shape[1])))
            alpha = jnp.exp(m_prev - m_next)
            l_ref[h, rows, :] = alpha * l_ref[h, rows, :] + jnp.sum(p, axis=1, keepdims=True)
            m_ref[h, rows, :] = m_next
            pv = jnp.dot(p.astype(v.dtype), v, preferred_element_type=jnp.float32)
            alphas.append(alpha)
            pvs.append(pv)
        alpha_b = jnp.where(lane, alphas[0], alphas[1])
        pv_b = jnp.where(lane, pvs[0], pvs[1])
        acc_ref[rows, :] = alpha_b * acc_ref[rows, :] + pv_b

    @pl.when(active)
    def _():
        for r in range(rows_all // ROW_BLOCK):
            qk_off = scal_ref[0] if r < half_blocks else scal_ref[1]
            dmin = qk_off + r * ROW_BLOCK - (t * tk + tk - 1)
            dmax = qk_off + r * ROW_BLOCK + ROW_BLOCK - 1 - t * tk

            @pl.when(dmin >= far_edge)
            def _():
                update(r, False, qk_off)

            @pl.when((dmin < far_edge) & (dmax >= 0))
            def _():
                update(r, True, qk_off)


def attend(state, q, keys, values, offsets, n_valid, skip, dtab):
    m, l, acc = state
    rows, width = q.shape
    n_tiles = keys.shape[0] // KEY_TILE
    scal = jnp.stack(
        [jnp.asarray(x, jnp.int32) for x in (offsets[0], offsets[1], n_valid, skip[0], skip[1])]
    )

    def tile_map(t, sc):
        return (jnp.maximum(jnp.minimum(t, sc[2] - 1), 0), 0)

    full2 = lambda t, sc: (0, 0)
    full3 = lambda t, sc: (0, 0, 0)
    flops = 8 * rows * KEY_TILE * width * n_tiles * 2
    cost = pl.CostEstimate(
        flops=flops,
        transcendentals=2 * rows * KEY_TILE * n_tiles,
        bytes_accessed=2 * keys.size * 2 + 6 * rows * width * 4,
    )
    return pl.pallas_call(
        attn_kernel,
        out_shape=(
            jax.ShapeDtypeStruct(m.shape, jnp.float32),
            jax.ShapeDtypeStruct(l.shape, jnp.float32),
            jax.ShapeDtypeStruct(acc.shape, jnp.float32),
        ),
        grid_spec=pltpu.PrefetchScalarGridSpec(
            num_scalar_prefetch=1,
            grid=(n_tiles,),
            in_specs=[
                pl.BlockSpec(memory_space=pltpu.SMEM),
                pl.BlockSpec((rows, width), full2),
                pl.BlockSpec((KEY_TILE, width), tile_map),
                pl.BlockSpec((KEY_TILE, width), tile_map),
                pl.BlockSpec(m.shape, full3),
                pl.BlockSpec(l.shape, full3),
                pl.BlockSpec(acc.shape, full2),
            ],
            out_specs=[
                pl.BlockSpec(m.shape, full3),
                pl.BlockSpec(l.shape, full3),
                pl.BlockSpec(acc.shape, full2),
            ],
        ),
        compiler_params=pltpu.CompilerParams(dimension_semantics=("arbitrary",)),
        cost_estimate=cost,
    )(scal, dtab, q, keys, values, m, l, acc)


def rms_scale(rows, gain):
    return (
        rows * lax.rsqrt(jnp.mean(rows * rows, axis=-1, keepdims=True) + epsilon) * gain
    ).astype(jnp.bfloat16)


def per_device(
    layer_input,
    queries,
    fresh_keys,
    fresh_values,
    cached_keys,
    cached_values,
    start_position,
    bias_table,
    out_weight,
    norm_gain,
    routes,
    route_weights,
    expert_in,
    expert_out,
):
    tok_rows = queries.shape[0]
    width = queries.shape[1]
    half = tok_rows // 2
    offset = start_position[0]
    n_seq = lax.axis_size("seq")
    seq_index = lax.axis_index("seq")
    partner = n_seq - 1 - seq_index
    swap = [(i, n_seq - 1 - i) for i in range(n_seq)]
    rows_q = jnp.concatenate([queries[:half], lax.ppermute(queries[half:], "seq", swap)], 0)
    dtab = bias_table - bias_table[bias_table.shape[0] - 1][None, :]
    state = (
        jnp.full((2, tok_rows, 128), lowest, jnp.float32),
        jnp.zeros((2, tok_rows, 128), jnp.float32),
        jnp.zeros((tok_rows, width), jnp.float32),
    )
    own_tiles = fresh_keys.shape[0] // KEY_TILE
    no_skip = (0, 0)
    state = attend(
        state,
        rows_q,
        fresh_keys,
        fresh_values,
        (0, (partner - seq_index) * tok_rows),
        own_tiles,
        no_skip,
        dtab,
    )
    prior_k = lax.all_gather(cached_keys, "seq", axis=0, tiled=True)
    prior_v = lax.all_gather(cached_values, "seq", axis=0, tiled=True)
    state = attend(
        state,
        rows_q,
        prior_k,
        prior_v,
        (offset + seq_index * tok_rows, offset + partner * tok_rows),
        prior_k.shape[0] // KEY_TILE,
        no_skip,
        dtab,
    )
    all_k = lax.all_gather(fresh_keys, "seq", axis=0, tiled=True)
    all_v = lax.all_gather(fresh_values, "seq", axis=0, tiled=True)
    state = attend(
        state,
        rows_q,
        all_k,
        all_v,
        (seq_index * tok_rows, partner * tok_rows),
        jnp.maximum(seq_index * own_tiles + own_tiles // 2, (partner + 1) * own_tiles),
        (seq_index * own_tiles, (seq_index + 1) * own_tiles),
        dtab,
    )
    m, l, acc = state
    lane = lax.broadcasted_iota(jnp.int32, (1, width), 1) < HEAD_DIM
    totals = jnp.where(lane, l[0], l[1])
    done_rows = (acc / totals).astype(jnp.bfloat16)
    attended = jnp.concatenate([done_rows[:half], lax.ppermute(done_rows[half:], "seq", swap)], 0)
    attended_full = lax.all_gather(attended, "tensor", axis=1, tiled=True)
    weight_full = lax.all_gather(out_weight, "tensor", axis=0, tiled=True)
    col_width = D // lax.axis_size("tensor")
    col_start = lax.axis_index("tensor") * col_width
    resid = layer_input.astype(jnp.float32) + jnp.dot(
        attended_full, weight_full, preferred_element_type=jnp.float32
    )
    normed = rms_scale(resid, norm_gain)
    resid_cols = lax.dynamic_slice_in_dim(resid, col_start, col_width, 1)
    expert_count = expert_in.shape[0]
    flat_routes = routes.reshape(-1)
    onehot = (flat_routes[:, None] == jnp.arange(expert_count, dtype=jnp.int32)[None, :]).astype(
        jnp.int32
    )
    before = jnp.cumsum(onehot, axis=0) - onehot
    slot = jnp.sum(before * onehot, axis=1)
    target = flat_routes * CAP + slot
    owner = jnp.arange(flat_routes.shape[0], dtype=jnp.int32) // TOP
    slot_owner = jnp.zeros((expert_count * CAP,), jnp.int32).at[target].set(owner)
    buffer = jnp.take(normed, slot_owner, axis=0).reshape(expert_count, CAP, D)
    gate_up = jnp.einsum("ecd,edgf->ecgf", buffer, expert_in, preferred_element_type=jnp.float32)
    hidden = (jax.nn.gelu(gate_up[:, :, 0], approximate=True) * gate_up[:, :, 1]).astype(
        jnp.bfloat16
    )
    expert_rows = jnp.einsum(
        "ecf,efd->ecd", hidden, expert_out, preferred_element_type=jnp.float32
    ).reshape(expert_count * CAP, D)
    picked = jnp.take(expert_rows, target, axis=0).reshape(tok_rows, TOP, D)
    combined = jnp.sum(picked * route_weights[:, :, None], axis=1)
    expert_cols = lax.psum_scatter(
        combined.astype(jnp.bfloat16), "tensor", scatter_dimension=1, tiled=True
    ).astype(jnp.float32)
    return (resid_cols + expert_cols).astype(jnp.bfloat16)


def solution(mesh):
    return jax.shard_map(
        per_device,
        mesh=mesh,
        in_specs=(
            P("seq", None),
            P("seq", "tensor"),
            P("seq", "tensor"),
            P("seq", "tensor"),
            P("seq", "tensor"),
            P("seq", "tensor"),
            P(),
            P(None, "tensor"),
            P("tensor", None),
            P(),
            P("seq", None),
            P("seq", None),
            P(None, None, None, "tensor"),
            P(None, "tensor", None),
        ),
        out_specs=P("seq", "tensor"),
        check_vma=False,
    )
```

profile of v0, /device:TPU:1, one launch (start us, length us, event | category | flops | bytes accessed | tf_op | source)
XLA Modules:
  0.0 617.1 jit_solution(3190958509538410773)
XLA Ops:
  6.5 0.7 all-gather.11.cloned.1.call-update
  7.3 0.7 all-gather.13.cloned.1.call-update
  8.1 0.7 all-gather.7.cloned.1.call-update
  8.8 0.5 all-gather.9.cloned.1.call-update
  9.4 1.0 fusion.38
  10.4 7.7 %collective-permute-start = (bf16[512,128]{1,0:T(8,128)(2,1)S(1)}, bf16[512,128]{1,0:T(8,128)(2,1)S(1)}, u32[]{:S(2)}, u32[]{:S(2)}) collective-permute-start(bf16[512,128]{1,0:T(8,128)(2,1)S(1)} %get-tuple-element.24), channel_id=1, source_target_pairs={{0,120},{8,112},{16,104},{24,96},{32,88},{40,80},{48,72},{56,64},{... | collective-permute-start | bytes 393224 | tf_op jit(solution)/shard_map/ppermute | solution.py:181
  18.1 0.8 copy.42
  18.9 0.9 slice_reduce_fusion.1
  19.7 0.6 broadcast_subtract_fusion.dtab_ref
  21.0 0.6 stack.38.scal_ref
  21.6 0.7 pad_add_fusion
  22.3 0.7 pad_maximum_fusion.q_ref
  23.0 1.0 broadcast_in_dim.49.m_in
  24.0 1.1 broadcast_in_dim.50.l_in
  25.1 0.8 broadcast_in_dim.51.acc_in
  26.0 19.3 %shard_map.136 = (f32[2,1024,128]{2,1,0:T(8,128)}, f32[2,1024,128]{2,1,0:T(8,128)}, f32[1024,128]{1,0:T(8,128)}) custom-call(s32[5]{0:T(128)} %get-tuple-element.25.scal_ref, f32[32,2]{1,0:T(8,128)} %broadcast_subtract_fusion.dtab_ref, bf16[1024,128]{1,0:T(8,128)(2,1)} %pad_maximum_fusion.q_ref, bf16[1024,128]{1,0:T(8,128)(2,1)} %k_ref.1, ...), custom_call_target="tpu_custom_call" | custom-call | flops 2147483648 | bytes 3670016 | tf_op jit(solution)/shard_map/pallas_call | solution.py:121
  45.3 18.9 %all-gather.11.cloned.1.call-done.k_ref = bf16[12288,128]{1,0:T(8,128)(2,1)} async-done(((bf16[768,128]{1,0:T(8,128)(2,1)}), bf16[12288,128]{1,0:T(8,128)(2,1)}) %all-gather.11.cloned.1.call-update) | async-done | bytes 3145744 | tf_op jit(solution)/shard_map/all_gather | solution.py:200
  64.1 51.9 %all-gather.13.cloned.1.call-done.v_ref = bf16[12288,128]{1,0:T(8,128)(2,1)} async-done(((bf16[768,128]{1,0:T(8,128)(2,1)}), bf16[12288,128]{1,0:T(8,128)(2,1)}) %all-gather.13.cloned.1.call-update) | async-done | bytes 3145744 | tf_op jit(solution)/shard_map/all_gather | solution.py:201
  116.1 153.6 %shard_map.137 = (f32[2,1024,128]{2,1,0:T(8,128)}, f32[2,1024,128]{2,1,0:T(8,128)}, f32[1024,128]{1,0:T(8,128)}) custom-call(s32[5]{0:T(128)} %get-tuple-element.26.scal_ref, f32[32,2]{1,0:T(8,128)} %broadcast_subtract_fusion.dtab_ref, bf16[1024,128]{1,0:T(8,128)(2,1)} %pad_maximum_fusion.q_ref, bf16[12288,128]{1,0:T(8,128)(2,1)} %all-gather.11.cloned.1.call-done.k_ref, ...), custom_call_target="tpu_custom_call" | custom-call | flops 25769803776 | bytes 9437184 | tf_op jit(solution)/shard_map/pallas_call | solution.py:121
  269.7 116.9 %shard_map.138 = (f32[2,1024,128]{2,1,0:T(8,128)}, f32[2,1024,128]{2,1,0:T(8,128)}, f32[1024,128]{1,0:T(8,128)}) custom-call(s32[5]{0:T(128)} %stack.38.scal_ref, f32[32,2]{1,0:T(8,128)} %broadcast_subtract_fusion.dtab_ref, bf16[1024,128]{1,0:T(8,128)(2,1)} %pad_maximum_fusion.q_ref, bf16[16384,128]{1,0:T(8,128)(2,1)} %all-gather.7.cloned.1.call-done.k_ref, ...), custom_call_target="tpu_custom_call" | custom-call | flops 34359738368 | bytes 11534336 | tf_op jit(solution)/shard_map/pallas_call | solution.py:121
  386.7 1.6 fusion.21
  388.3 6.9 %collective-permute-start.1 = (bf16[512,128]{1,0:T(8,128)(2,1)S(1)}, bf16[512,128]{1,0:T(8,128)(2,1)S(1)}, u32[]{:S(2)}, u32[]{:S(2)}) collective-permute-start(bf16[512,128]{1,0:T(8,128)(2,1)S(1)} %get-tuple-element.22), channel_id=1, source_target_pairs={{0,120},{8,112},{16,104},{24,96},{32,88},{40,80},{48,72},{56,64},{... | collective-permute-start | bytes 393224 | tf_op jit(solution)/shard_map/ppermute | solution.py:228
  395.1 3.9 collective-permute-done.1
  399.0 0.7 pad_maximum_fusion.1
  400.1 0.3 eq.26
  400.3 0.3 reshape.92
  400.6 2.6 copy.41
  403.2 2.3 reduce-window.6
  405.4 0.3 slice_reduce_fusion
  406.2 0.3 mul.107
  406.6 0.5 reduce_sum.32
  407.1 8.1 %scatter_custom_fusion = s32[3072]{0:T(1024)S(1)} fusion(s32[2048]{0:T(1024)S(1)} %bitcast.66, s32[2048]{0:T(1024)S(1)} %add_select_fusion, s32[]{:T(128)} %constant.47.clone.1), kind=kCustom, calls=%fused_computation.58 | custom fusion | bytes 12292 | tf_op jit(solution)/shard_map/scatter | solution.py:247
  415.4 0.3 copy.46
  416.0 33.7 %all-gather.15.cloned.1.call-done = bf16[1024,1024]{1,0:T(8,128)(2,1)} async-done(((bf16[1024,128]{1,0:T(8,128)(2,1)}), bf16[1024,1024]{1,0:T(8,128)(2,1)}) %all-gather.15.cloned.1.call-update) | async-done | bytes 2097168 | tf_op jit(solution)/shard_map/all_gather | solution.py:229
  449.7 5.4 multiply_reduce_fusion.1
  455.2 2.0 copy-done
  457.2 1.8 multiply_convert_fusion
  458.9 3.0 copy.48
  462.0 13.9 %gather_fusion = bf16[3072,1024]{1,0:T(8,128)(2,1)} fusion(bf16[1024,1024]{1,0:T(8,128)(2,1)S(1)} %copy.48, s32[3072]{0:T(1024)S(1)} %fusion.26), kind=kCustom, calls=%fused_computation | custom fusion | bytes 12595200 | tf_op jit(solution)/shard_map/jit(_take)/gather | solution.py:248
  475.9 15.6 %fusion = f32[8,384,2,352]{1,3,2,0:T(8,128)} fusion(bf16[8,1024,2,352]{1,3,2,0:T(8,128)(2,1)} %param.26, bf16[8,384,1024]{2,1,0:T(8,128)(2,1)} %bitcast.64, pred[8,384]{1,0:T(8,128)(4,1)S(1)} %broadcast_in_dim.55), kind=kOutput, calls=%fused_computation.5 | convolution fusion | flops 4432330752 | bytes 26479616 | tf_op jit(solution)/shard_map/ecd,edgf->ecgf/dot_general | solution.py:249
  491.4 13.3 %fusion.14 = f32[8,384,1024]{2,1,0:T(8,128)} fusion(bf16[8,352,1024]{2,1,0:T(8,128)(2,1)} %param.27, f32[8,384,2,352]{1,3,2,0:T(8,128)} %fusion), kind=kOutput, calls=%fused_computation.24 | convolution fusion | flops 2225405952 | bytes 27000832 | tf_op jit(solution)/shard_map/ecf,efd->ecd/dot_general | solution.py:253
  504.7 16.3 %gather_fusion.1 = f32[2048,1024]{1,0:T(8,128)} fusion(f32[3072,1024]{1,0:T(8,128)} %bitcast.63, s32[2048]{0:T(1024)S(1)} %broadcast_clamp_fusion), kind=kCustom, calls=%fused_computation.1 | custom fusion | bytes 16785408 | tf_op jit(solution)/shard_map/jit(_take)/gather | solution.py:256
  521.0 10.6 %gather.15 = f32[1024,2,1024]{2,1,0:T(2,128)} reshape(f32[2048,1024]{1,0:T(8,128)} %gather_fusion.1) | data formatting | bytes 16777216 | tf_op jit(solution)/shard_map/jit(_take)/gather | solution.py:256
  531.6 17.5 %multiply_reduce_fusion = bf16[1024,1024]{1,0:T(8,128)(2,1)S(1)} fusion(f32[1024,2,1024]{2,1,0:T(2,128)} %gather.15, pred[1024,2]{1,0:T(8,128)(4,1)S(1)} %copy.46, f32[1024,2]{1,0:T(8,128)S(1)} %copy.50), kind=kLoop, calls=%fused_computation.3 | loop fusion | flops 5242880 | bytes 10496000 | tf_op jit(solution)/shard_map/reduce_sum | solution.py:257
  549.1 2.6 copy.51
  551.7 56.3 %reduce-scatter.2.cloned.1.call-done = bf16[1024,128]{0,1:T(8,128)(2,1)} async-done(((bf16[1024,1024]{0,1:T(8,128)(2,1)}), bf16[1024,128]{0,1:T(8,128)(2,1)}) %reduce-scatter.2.cloned.1.call-update) | async-done | bytes 262160 | tf_op jit(solution)/shard_map/reduce_scatter | solution.py:258
  607.9 1.2 add_convert_fusion
  609.1 0.8 copy.52
  (43 shorter events, 1.6 us)
Async XLA Ops:
  6.5 57.6 %all-gather.11.cloned.1.call-start = ((), (), s32[]{:S(2)}) async-start(), calls=%async_computation.3 | async-start | bytes 3342336 | tf_op jit(solution)/shard_map/all_gather | solution.py:200
  7.3 108.8 %all-gather.13.cloned.1.call-start = ((), (), s32[]{:S(2)}) async-start(), calls=%async_computation.4 | async-start | bytes 3342336 | tf_op jit(solution)/shard_map/all_gather | solution.py:201
  8.0 261.7 %all-gather.7.cloned.1.call-start = ((), (), s32[]{:S(2)}) async-start(), calls=%async_computation.1 | async-start | bytes 4456448 | tf_op jit(solution)/shard_map/all_gather | solution.py:212
  8.7 261.0 %all-gather.9.cloned.1.call-start = ((), (), s32[]{:S(2)}) async-start(), calls=%async_computation.2 | async-start | bytes 4456448 | tf_op jit(solution)/shard_map/all_gather | solution.py:213
  9.3 406.7 %all-gather.17.cloned.1.call-start = ((), (), s32[]{:S(2)}) async-start(), calls=%async_computation.6 | async-start | bytes 2359296 | tf_op jit(solution)/shard_map/all_gather | solution.py:230
  10.4 11.9 %collective-permute-start = (bf16[512,128]{1,0:T(8,128)(2,1)S(1)}, bf16[512,128]{1,0:T(8,128)(2,1)S(1)}, u32[]{:S(2)}, u32[]{:S(2)}) collective-permute-start(bf16[512,128]{1,0:T(8,128)(2,1)S(1)} %get-tuple-element.24), channel_id=1, source_target_pairs={{0,120},{8,112},{16,104},{24,96},{32,88},{40,80},{48,72},{56,64},{... | collective-permute-start | bytes 393224 | tf_op jit(solution)/shard_map/ppermute | solution.py:181
  18.1 431.7 %all-gather.15.cloned.1.call-start = ((), (), s32[]{:S(2)}) async-start(), calls=%async_computation.5 | async-start | bytes 2359296 | tf_op jit(solution)/shard_map/all_gather | solution.py:229
  269.7 130.1 %copy-start.2 = (s32[1024,2]{0,1:T(2,128)S(1)}, s32[1024,2]{0,1:T(2,128)}, u32[]{:S(2)}) copy-start(s32[1024,2]{0,1:T(2,128)} %param.24) | copy-start | bytes 24580
  386.6 13.9 %copy-start.1 = (bf16[1024,1024]{1,0:T(8,128)(2,1)S(1)}, bf16[1024,1024]{1,0:T(8,128)(2,1)}, u32[]{:S(2)}) copy-start(bf16[1024,1024]{1,0:T(8,128)(2,1)} %param.14) | copy-start | bytes 6291460
  388.3 10.7 %collective-permute-start.1 = (bf16[512,128]{1,0:T(8,128)(2,1)S(1)}, bf16[512,128]{1,0:T(8,128)(2,1)S(1)}, u32[]{:S(2)}, u32[]{:S(2)}) collective-permute-start(bf16[512,128]{1,0:T(8,128)(2,1)S(1)} %get-tuple-element.22), channel_id=1, source_target_pairs={{0,120},{8,112},{16,104},{24,96},{32,88},{40,80},{48,72},{56,64},{... | collective-permute-start | bytes 393224 | tf_op jit(solution)/shard_map/ppermute | solution.py:228
  399.8 16.0 %copy-start.3 = (f32[1024,2]{0,1:T(2,128)S(1)}, f32[1024,2]{0,1:T(2,128)}, u32[]{:S(2)}) copy-start(f32[1024,2]{0,1:T(2,128)} %param.25) | copy-start | bytes 24580
  399.8 208.2 %reduce-scatter.2.cloned.1.call-start = ((), (), s32[]{:S(2)}) async-start(), calls=%async_computation.7 | async-start | bytes 2359296 | tf_op jit(solution)/shard_map/reduce_scatter | solution.py:258
  416.0 41.2 %copy-start.4 = (f32[1024]{0:T(1024)S(1)}, f32[1024]{0:T(1024)}, u32[]{:S(2)}) copy-start(f32[1024]{0:T(1024)} %param.23) | copy-start | bytes 12292
  455.2 2.0 copy-start
Sparse Core Ops, SparseCore 0:
  9.8 54.2 all-gather.10
  66.6 49.3 all-gather.12
  118.5 53.9 all-gather.6
  174.8 52.7 all-gather.8
  229.1 48.8 all-gather.16
  399.9 49.7 all-gather.14
  551.8 56.0 reduce-scatter.1
where the time goes:
time: 618 us; the launch traced here: 617 us
  Pallas kernels  290 us (47%)
  waiting for transfers between devices  167 us (27%)
  local copies, waits for them, and re-layouts  68.8 us (11%)
  matrix products  34.3 us (6%)
  other arithmetic  27.4 us (4%)
  starting transfers between devices  14.8 us (2%)
  between operations  14.7 us (2%)
    pallas_call x3, Pallas kernels, attend(): pl.pallas_call(attn_kernel, out_shape=(jax.ShapeDtypeStruct(m.shape, jnp....  290 us
    reduce_scatter x1, waiting for transfers between devices, per_device(): lax.psum_scatter(combined.astype(jnp.bfloat16), 'tensor', scatter_dimensi...  56.3 us
    all_gather x1, waiting for transfers between devices, per_device(): prior_v = lax.all_gather(cached_values, 'seq', axis=0, tiled=True)  51.9 us
    all_gather x1, waiting for transfers between devices, per_device(): attended_full = lax.all_gather(attended, 'tensor', axis=1, tiled=True)  33.7 us
    gather x2, local copies, waits for them, and re-layouts, per_device(): picked = jnp.take(expert_rows, target, axis=0).reshape(tok_rows, TOP, D)  26.8 us
    all_gather x1, waiting for transfers between devices, per_device(): prior_k = lax.all_gather(cached_keys, 'seq', axis=0, tiled=True)  18.9 us
    reduce_sum x1, other arithmetic, per_device(): combined = jnp.sum(picked * route_weights[:, :, None], axis=1)  17.5 us
    dot_general x1, matrix products, per_device(): jnp.einsum('ecd,edgf->ecgf', buffer, expert_in, preferred_element_type=jn...  15.6 us
  transfers between devices with their start and end apart: 9, of which 5 were waited for; matrix products, arithmetic and copies ran while one was open for 4% of the time, Pallas kernels for 47%

commit v1 on v0

--- a/solution.py
+++ b/solution.py
@@ -35,6 +35,7 @@
         acc_ref[...] = acc_in[...]
 
     n_valid = scal_ref[2]
+    stride = scal_ref[5]
     active = (t < n_valid) & ((t < scal_ref[3]) | (t >= scal_ref[4]))
     half_blocks = rows_all // ROW_BLOCK // 2
 
@@ -46,7 +47,7 @@
         lane = lax.broadcasted_iota(jnp.int32, (1, q.shape[1]), 1) < HEAD_DIM
         zero_q = jnp.zeros_like(q)
         if near:
-            base = qk_off + r * ROW_BLOCK - t * tk
+            base = qk_off + r * ROW_BLOCK - t * stride
             d = (
                 base
                 + lax.broadcasted_iota(jnp.int32, (ROW_BLOCK, tk), 0)
@@ -87,8 +88,8 @@
     def _():
         for r in range(rows_all // ROW_BLOCK):
             qk_off = scal_ref[0] if r < half_blocks else scal_ref[1]
-            dmin = qk_off + r * ROW_BLOCK - (t * tk + tk - 1)
-            dmax = qk_off + r * ROW_BLOCK + ROW_BLOCK - 1 - t * tk
+            dmin = qk_off + r * ROW_BLOCK - (t * stride + tk - 1)
+            dmax = qk_off + r * ROW_BLOCK + ROW_BLOCK - 1 - t * stride
 
             @pl.when(dmin >= far_edge)
             def _():
@@ -99,12 +100,15 @@
                 update(r, True, qk_off)
 
 
-def attend(state, q, keys, values, offsets, n_valid, skip, dtab):
+def attend(state, q, keys, values, offsets, n_valid, skip, dtab, stride=KEY_TILE):
     m, l, acc = state
     rows, width = q.shape
     n_tiles = keys.shape[0] // KEY_TILE
     scal = jnp.stack(
-        [jnp.asarray(x, jnp.int32) for x in (offsets[0], offsets[1], n_valid, skip[0], skip[1])]
+        [
+            jnp.asarray(x, jnp.int32)
+            for x in (offsets[0], offsets[1], n_valid, skip[0], skip[1], stride)
+        ]
     )
 
     def tile_map(t, sc):
@@ -197,18 +201,22 @@
         no_skip,
         dtab,
     )
-    prior_k = lax.all_gather(cached_keys, "seq", axis=0, tiled=True)
-    prior_v = lax.all_gather(cached_values, "seq", axis=0, tiled=True)
-    state = attend(
-        state,
-        rows_q,
-        prior_k,
-        prior_v,
-        (offset + seq_index * tok_rows, offset + partner * tok_rows),
-        prior_k.shape[0] // KEY_TILE,
-        no_skip,
-        dtab,
-    )
+    prior_rows = cached_keys.shape[0]
+    split = prior_rows - KEY_TILE
+    for lo, hi in ((0, split), (split, prior_rows)):
+        prior_k = lax.all_gather(cached_keys[lo:hi], "seq", axis=0, tiled=True)
+        prior_v = lax.all_gather(cached_values[lo:hi], "seq", axis=0, tiled=True)
+        state = attend(
+            state,
+            rows_q,
+            prior_k,
+            prior_v,
+            (offset + seq_index * tok_rows - lo, offset + partner * tok_rows - lo),
+            prior_k.shape[0] // KEY_TILE,
+            no_skip,
+            dtab,
+            KEY_TILE if lo == 0 else prior_rows,
+        )
     all_k = lax.all_gather(fresh_keys, "seq", axis=0, tiled=True)
     all_v = lax.all_gather(fresh_values, "seq", axis=0, tiled=True)
     state = attend(

time: 618 us -> 660 us (1.068)
  Pallas kernels: 290 us -> 309 us
  waiting for transfers between devices: 167 us -> 185 us
  local copies, waits for them, and re-layouts: 68.8 us -> 76.9 us
    pallas_call x3 -> x4, Pallas kernels: 290 us -> 309 us  [attend(): pl.pallas_call(attn_kernel, out_shape=(jax.ShapeDtypeStruct(m.shape, jnp....]
    all_gather x2 -> x4, waiting for transfers between devices: 70.8 us -> 86.9 us  [the longest x2 79.9 us: per_device(): prior_v = lax.all_gather(cached_values[lo:hi], 'seq', axis=0, tiled=True)]
  transfers between devices with their start and end apart: 9 -> 11, of which waited for: 5 -> 7; matrix products, arithmetic and copies ran while one was open for 4% -> 5% of each run, Pallas kernels for 47% -> 47%
where the time goes in v1:
time: 660 us
  Pallas kernels  309 us (47%)
  waiting for transfers between devices  185 us (28%)
  local copies, waits for them, and re-layouts  76.9 us (12%)
  matrix products  34.3 us (5%)
  other arithmetic  26.8 us (4%)
  between operations  14.4 us (2%)
  starting transfers between devices  13.8 us (2%)
    pallas_call x4, Pallas kernels, attend(): pl.pallas_call(attn_kernel, out_shape=(jax.ShapeDtypeStruct(m.shape, jnp....  309 us
    all_gather x2, waiting for transfers between devices, per_device(): prior_v = lax.all_gather(cached_values[lo:hi], 'seq', axis=0, tiled=True)  79.9 us
    reduce_scatter x1, waiting for transfers between devices, per_device(): lax.psum_scatter(combined.astype(jnp.bfloat16), 'tensor', scatter_dimensi...  56.2 us
    all_gather x1, waiting for transfers between devices, per_device(): attended_full = lax.all_gather(attended, 'tensor', axis=1, tiled=True)  33.6 us
    gather x2, local copies, waits for them, and re-layouts, per_device(): picked = jnp.take(expert_rows, target, axis=0).reshape(tok_rows, TOP, D)  26.9 us
    reduce_sum x1, other arithmetic, per_device(): combined = jnp.sum(picked * route_weights[:, :, None], axis=1)  17.5 us
    dot_general x1, matrix products, per_device(): jnp.einsum('ecd,edgf->ecgf', buffer, expert_in, preferred_element_type=jn...  15.6 us
    gather x1, local copies, waits for them, and re-layouts, per_device(): buffer = jnp.take(normed, slot_owner, axis=0).reshape(expert_count, CAP, D)  14 us
  transfers between devices with their start and end apart: 11, of which 7 were waited for; matrix products, arithmetic and copies ran while one was open for 5% of the time, Pallas kernels for 47%

profile of v1, /device:TPU:1, one launch (start us, length us, event | category | flops | bytes accessed | tf_op | source)
XLA Modules:
  0.0 659.7 jit_solution(10246414763243374809)
XLA Ops:
  6.5 1.5 slice.50
  8.1 1.5 slice.51
  9.6 1.6 slice.48
  11.3 1.6 slice.49
  12.9 0.5 all-gather.11.cloned.1.call-update
  14.1 1.0 fusion.38
  15.1 7.7 %collective-permute-start = (bf16[512,128]{1,0:T(8,128)(2,1)S(1)}, bf16[512,128]{1,0:T(8,128)(2,1)S(1)}, u32[]{:S(2)}, u32[]{:S(2)}) collective-permute-start(bf16[512,128]{1,0:T(8,128)(2,1)S(1)} %get-tuple-element.30), channel_id=1, source_target_pairs={{0,120},{8,112},{16,104},{24,96},{32,88},{40,80},{48,72},{56,64},{... | collective-permute-start | bytes 393224 | tf_op jit(solution)/shard_map/ppermute | solution.py:185
  22.8 0.8 copy.42
  23.6 0.9 slice_reduce_fusion.1
  24.4 0.6 broadcast_subtract_fusion.dtab_ref
  25.7 0.6 stack.55.scal_ref
  26.3 0.6 stack.53.scal_ref
  26.9 0.6 stack.50.scal_ref
  27.6 0.7 stack.47.scal_ref
  28.2 0.7 pad_maximum_fusion.q_ref
  29.0 1.0 broadcast_in_dim.49.m_in
  30.0 1.1 broadcast_in_dim.50.l_in
  31.1 0.8 broadcast_in_dim.51.acc_in
  31.9 19.3 %shard_map.136 = (f32[2,1024,128]{2,1,0:T(8,128)}, f32[2,1024,128]{2,1,0:T(8,128)}, f32[1024,128]{1,0:T(8,128)}) custom-call(s32[6]{0:T(128)} %stack.55.scal_ref, f32[32,2]{1,0:T(8,128)} %broadcast_subtract_fusion.dtab_ref, bf16[1024,128]{1,0:T(8,128)(2,1)} %pad_maximum_fusion.q_ref, bf16[1024,128]{1,0:T(8,128)(2,1)} %k_ref.1, bf16[1024,128]{1,0:T(8,128)(2,1)} %v_ref.1, ...), custom_call_target="tpu_custom_call" | custom-call | flops 2147483648 | bytes 3670016 | tf_op jit(solution)/shard_map/pallas_call | solution.py:125
  51.2 7.0 %all-gather.17.cloned.1.call-done.k_ref = bf16[4096,128]{1,0:T(8,128)(2,1)} async-done(((bf16[256,128]{1,0:T(8,128)(2,1)}), bf16[4096,128]{1,0:T(8,128)(2,1)}) %all-gather.17.cloned.1.call-update) | async-done | bytes 1048592 | tf_op jit(solution)/shard_map/all_gather | solution.py:207
  58.2 46.1 %all-gather.19.cloned.1.call-done.v_ref = bf16[4096,128]{1,0:T(8,128)(2,1)} async-done(((bf16[256,128]{1,0:T(8,128)(2,1)}), bf16[4096,128]{1,0:T(8,128)(2,1)}) %all-gather.19.cloned.1.call-update) | async-done | bytes 1048592 | tf_op jit(solution)/shard_map/all_gather | solution.py:208
  104.3 63.8 %shard_map.137 = (f32[2,1024,128]{2,1,0:T(8,128)}, f32[2,1024,128]{2,1,0:T(8,128)}, f32[1024,128]{1,0:T(8,128)}) custom-call(s32[6]{0:T(128)} %stack.53.scal_ref, f32[32,2]{1,0:T(8,128)} %broadcast_subtract_fusion.dtab_ref, bf16[1024,128]{1,0:T(8,128)(2,1)} %pad_maximum_fusion.q_ref, bf16[4096,128]{1,0:T(8,128)(2,1)} %all-gather.17.cloned.1.call-done.k_ref, ...), custom_call_target="tpu_custom_call" | custom-call | flops 8589934592 | bytes 5242880 | tf_op jit(solution)/shard_map/pallas_call | solution.py:125
  168.2 33.8 %all-gather.15.cloned.1.call-done.v_ref = bf16[8192,128]{1,0:T(8,128)(2,1)} async-done(((bf16[512,128]{1,0:T(8,128)(2,1)}), bf16[8192,128]{1,0:T(8,128)(2,1)}) %all-gather.15.cloned.1.call-update) | async-done | bytes 2097168 | tf_op jit(solution)/shard_map/all_gather | solution.py:208
  201.9 108.8 %shard_map.138 = (f32[2,1024,128]{2,1,0:T(8,128)}, f32[2,1024,128]{2,1,0:T(8,128)}, f32[1024,128]{1,0:T(8,128)}) custom-call(s32[6]{0:T(128)} %stack.50.scal_ref, f32[32,2]{1,0:T(8,128)} %broadcast_subtract_fusion.dtab_ref, bf16[1024,128]{1,0:T(8,128)(2,1)} %pad_maximum_fusion.q_ref, bf16[8192,128]{1,0:T(8,128)(2,1)} %all-gather.13.cloned.1.call-done.k_ref, ...), custom_call_target="tpu_custom_call" | custom-call | flops 17179869184 | bytes 7340032 | tf_op jit(solution)/shard_map/pallas_call | solution.py:125
  310.7 2.7 all-gather.9.cloned.1.call-done.k_ref
  313.4 117.0 %shard_map.139 = (f32[2,1024,128]{2,1,0:T(8,128)}, f32[2,1024,128]{2,1,0:T(8,128)}, f32[1024,128]{1,0:T(8,128)}) custom-call(s32[6]{0:T(128)} %stack.47.scal_ref, f32[32,2]{1,0:T(8,128)} %broadcast_subtract_fusion.dtab_ref, bf16[1024,128]{1,0:T(8,128)(2,1)} %pad_maximum_fusion.q_ref, bf16[16384,128]{1,0:T(8,128)(2,1)} %all-gather.9.cloned.1.call-done.k_ref, ...), custom_call_target="tpu_custom_call" | custom-call | flops 34359738368 | bytes 11534336 | tf_op jit(solution)/shard_map/pallas_call | solution.py:125
  430.5 1.6 fusion.21
  432.1 5.8 collective-permute-start.1
  437.9 3.9 collective-permute-done.1
  441.8 0.7 pad_maximum_fusion.1
  443.4 2.6 copy.41
  446.0 2.3 reduce-window.6
  449.9 8.1 %scatter_custom_fusion = s32[3072]{0:T(1024)S(1)} fusion(s32[2048]{0:T(1024)S(1)} %bitcast.68, s32[2048]{0:T(1024)S(1)} %add_select_fusion, s32[]{:T(128)} %constant.51.clone.1), kind=kCustom, calls=%fused_computation.58 | custom fusion | bytes 12292 | tf_op jit(solution)/shard_map/scatter | solution.py:255
  458.8 33.6 %all-gather.21.cloned.1.call-done = bf16[1024,1024]{1,0:T(8,128)(2,1)} async-done(((bf16[1024,128]{1,0:T(8,128)(2,1)}), bf16[1024,1024]{1,0:T(8,128)(2,1)}) %all-gather.21.cloned.1.call-update) | async-done | bytes 2097168 | tf_op jit(solution)/shard_map/all_gather | solution.py:237
  492.4 5.4 multiply_reduce_fusion.1
  497.9 2.0 copy-done
  499.9 1.8 multiply_convert_fusion
  501.7 3.0 copy.48
  504.7 14.0 %gather_fusion = bf16[3072,1024]{1,0:T(8,128)(2,1)} fusion(bf16[1024,1024]{1,0:T(8,128)(2,1)S(1)} %copy.48, s32[3072]{0:T(1024)S(1)} %fusion.26), kind=kCustom, calls=%fused_computation | custom fusion | bytes 12595200 | tf_op jit(solution)/shard_map/jit(_take)/gather | solution.py:256
  518.7 15.6 %fusion = f32[8,384,2,352]{1,3,2,0:T(8,128)} fusion(bf16[8,1024,2,352]{1,3,2,0:T(8,128)(2,1)} %param.26, bf16[8,384,1024]{2,1,0:T(8,128)(2,1)} %bitcast.66, pred[8,384]{1,0:T(8,128)(4,1)S(1)} %broadcast_in_dim.55), kind=kOutput, calls=%fused_computation.5 | convolution fusion | flops 4432330752 | bytes 26479616 | tf_op jit(solution)/shard_map/ecd,edgf->ecgf/dot_general | solution.py:257
  534.3 13.3 %fusion.14 = f32[8,384,1024]{2,1,0:T(8,128)} fusion(bf16[8,352,1024]{2,1,0:T(8,128)(2,1)} %param.27, f32[8,384,2,352]{1,3,2,0:T(8,128)} %fusion), kind=kOutput, calls=%fused_computation.24 | convolution fusion | flops 2225405952 | bytes 27000832 | tf_op jit(solution)/shard_map/ecf,efd->ecd/dot_general | solution.py:261
  547.6 16.3 %gather_fusion.1 = f32[2048,1024]{1,0:T(8,128)} fusion(f32[3072,1024]{1,0:T(8,128)} %bitcast.65, s32[2048]{0:T(1024)S(1)} %broadcast_clamp_fusion), kind=kCustom, calls=%fused_computation.1 | custom fusion | bytes 16785408 | tf_op jit(solution)/shard_map/jit(_take)/gather | solution.py:264
  563.9 10.6 %gather.15 = f32[1024,2,1024]{2,1,0:T(2,128)} reshape(f32[2048,1024]{1,0:T(8,128)} %gather_fusion.1) | data formatting | bytes 16777216 | tf_op jit(solution)/shard_map/jit(_take)/gather | solution.py:264
  574.5 17.5 %multiply_reduce_fusion = bf16[1024,1024]{1,0:T(8,128)(2,1)S(1)} fusion(f32[1024,2,1024]{2,1,0:T(2,128)} %gather.15, pred[1024,2]{1,0:T(8,128)(4,1)S(1)} %copy.46, f32[1024,2]{1,0:T(8,128)S(1)} %copy.50), kind=kLoop, calls=%fused_computation.3 | loop fusion | flops 5242880 | bytes 10496000 | tf_op jit(solution)/shard_map/reduce_sum | solution.py:265
  592.0 2.6 copy.51
  594.6 56.2 %reduce-scatter.2.cloned.1.call-done = bf16[1024,128]{0,1:T(8,128)(2,1)} async-done(((bf16[1024,1024]{0,1:T(8,128)(2,1)}), bf16[1024,128]{0,1:T(8,128)(2,1)}) %reduce-scatter.2.cloned.1.call-update) | async-done | bytes 262160 | tf_op jit(solution)/shard_map/reduce_scatter | solution.py:266
  650.8 1.2 add_convert_fusion
  652.0 0.8 copy.52
  (56 shorter events, 4.2 us)
Async XLA Ops:
  6.5 51.7 %all-gather.17.cloned.1.call-start = ((), (), s32[]{:S(2)}) async-start(), calls=%async_computation.5 | async-start | bytes 1114112 | tf_op jit(solution)/shard_map/all_gather | solution.py:207
  8.0 96.3 %all-gather.19.cloned.1.call-start = ((), (), s32[]{:S(2)}) async-start(), calls=%async_computation.6 | async-start | bytes 1114112 | tf_op jit(solution)/shard_map/all_gather | solution.py:208
  9.6 158.6 %all-gather.13.cloned.1.call-start = ((), (), s32[]{:S(2)}) async-start(), calls=%async_computation.3 | async-start | bytes 2228224 | tf_op jit(solution)/shard_map/all_gather | solution.py:207
  11.2 190.7 %all-gather.15.cloned.1.call-start = ((), (), s32[]{:S(2)}) async-start(), calls=%async_computation.4 | async-start | bytes 2228224 | tf_op jit(solution)/shard_map/all_gather | solution.py:208
  12.9 297.9 %all-gather.11.cloned.1.call-start = ((), (), s32[]{:S(2)}) async-start(), calls=%async_computation.2 | async-start | bytes 4456448 | tf_op jit(solution)/shard_map/all_gather | solution.py:221
  13.4 300.0 %all-gather.9.cloned.1.call-start = ((), (), s32[]{:S(2)}) async-start(), calls=%async_computation.1 | async-start | bytes 4456448 | tf_op jit(solution)/shard_map/all_gather | solution.py:220
  14.0 444.8 %all-gather.23.cloned.1.call-start = ((), (), s32[]{:S(2)}) async-start(), calls=%async_computation.8 | async-start | bytes 2359296 | tf_op jit(solution)/shard_map/all_gather | solution.py:238
  15.1 13.2 %collective-permute-start = (bf16[512,128]{1,0:T(8,128)(2,1)S(1)}, bf16[512,128]{1,0:T(8,128)(2,1)S(1)}, u32[]{:S(2)}, u32[]{:S(2)}) collective-permute-start(bf16[512,128]{1,0:T(8,128)(2,1)S(1)} %get-tuple-element.30), channel_id=1, source_target_pairs={{0,120},{8,112},{16,104},{24,96},{32,88},{40,80},{48,72},{56,64},{... | collective-permute-start | bytes 393224 | tf_op jit(solution)/shard_map/ppermute | solution.py:185
  22.8 469.7 %all-gather.21.cloned.1.call-start = ((), (), s32[]{:S(2)}) async-start(), calls=%async_computation.7 | async-start | bytes 2359296 | tf_op jit(solution)/shard_map/all_gather | solution.py:237
  313.4 129.2 %copy-start.2 = (s32[1024,2]{0,1:T(2,128)S(1)}, s32[1024,2]{0,1:T(2,128)}, u32[]{:S(2)}) copy-start(s32[1024,2]{0,1:T(2,128)} %param.24) | copy-start | bytes 24580
  430.4 12.9 %copy-start.1 = (bf16[1024,1024]{1,0:T(8,128)(2,1)S(1)}, bf16[1024,1024]{1,0:T(8,128)(2,1)}, u32[]{:S(2)}) copy-start(bf16[1024,1024]{1,0:T(8,128)(2,1)} %param.14) | copy-start | bytes 6291460
  432.1 9.7 %collective-permute-start.1 = (bf16[512,128]{1,0:T(8,128)(2,1)S(1)}, bf16[512,128]{1,0:T(8,128)(2,1)S(1)}, u32[]{:S(2)}, u32[]{:S(2)}) collective-permute-start(bf16[512,128]{1,0:T(8,128)(2,1)S(1)} %get-tuple-element.28), channel_id=1, source_target_pairs={{0,120},{8,112},{16,104},{24,96},{32,88},{40,80},{48,72},{56,64},{... | collective-permute-start | bytes 393224 | tf_op jit(solution)/shard_map/ppermute | solution.py:236
  442.5 16.0 %copy-start.3 = (f32[1024,2]{0,1:T(2,128)S(1)}, f32[1024,2]{0,1:T(2,128)}, u32[]{:S(2)}) copy-start(f32[1024,2]{0,1:T(2,128)} %param.25) | copy-start | bytes 24580
  442.5 208.3 %reduce-scatter.2.cloned.1.call-start = ((), (), s32[]{:S(2)}) async-start(), calls=%async_computation.9 | async-start | bytes 2359296 | tf_op jit(solution)/shard_map/reduce_scatter | solution.py:266
  458.8 41.1 %copy-start.4 = (f32[1024]{0:T(1024)S(1)}, f32[1024]{0:T(1024)}, u32[]{:S(2)}) copy-start(f32[1024]{0:T(1024)} %param.23) | copy-start | bytes 12292
  497.9 2.0 copy-start
Sparse Core Ops, SparseCore 0:
  9.8 48.3 all-gather.16
  60.7 43.6 all-gather.18
  106.8 46.5 all-gather.12
  155.7 46.1 all-gather.14
  204.3 53.8 all-gather.10
  260.4 52.9 all-gather.8
  315.1 48.6 all-gather.22
  442.6 49.7 all-gather.20
  594.8 56.0 reduce-scatter.1

commit v2 on v0

--- a/solution.py
+++ b/solution.py
@@ -99,16 +99,19 @@
                 update(r, True, qk_off)
 
 
-def attend(state, q, keys, values, offsets, n_valid, skip, dtab):
+def attend(state, q, pairs, offsets, n_valid, skip, dtab):
     m, l, acc = state
     rows, width = q.shape
-    n_tiles = keys.shape[0] // KEY_TILE
+    n_tiles = pairs.shape[0] // KEY_TILE
     scal = jnp.stack(
         [jnp.asarray(x, jnp.int32) for x in (offsets[0], offsets[1], n_valid, skip[0], skip[1])]
     )
 
-    def tile_map(t, sc):
-        return (jnp.maximum(jnp.minimum(t, sc[2] - 1), 0), 0)
+    def tile_index(t, sc):
+        return jnp.maximum(jnp.minimum(t, sc[2] - 1), 0)
+
+    key_map = lambda t, sc: (tile_index(t, sc), 0)
+    value_map = lambda t, sc: (tile_index(t, sc), 1)
 
     full2 = lambda t, sc: (0, 0)
     full3 = lambda t, sc: (0, 0, 0)
@@ -116,7 +119,7 @@
     cost = pl.CostEstimate(
         flops=flops,
         transcendentals=2 * rows * KEY_TILE * n_tiles,
-        bytes_accessed=2 * keys.size * 2 + 6 * rows * width * 4,
+        bytes_accessed=pairs.size * 2 + 6 * rows * width * 4,
     )
     return pl.pallas_call(
         attn_kernel,
@@ -131,8 +134,8 @@
             in_specs=[
                 pl.BlockSpec(memory_space=pltpu.SMEM),
                 pl.BlockSpec((rows, width), full2),
-                pl.BlockSpec((KEY_TILE, width), tile_map),
-                pl.BlockSpec((KEY_TILE, width), tile_map),
+                pl.BlockSpec((KEY_TILE, width), key_map),
+                pl.BlockSpec((KEY_TILE, width), value_map),
                 pl.BlockSpec(m.shape, full3),
                 pl.BlockSpec(l.shape, full3),
                 pl.BlockSpec(acc.shape, full2),
@@ -145,7 +148,7 @@
         ),
         compiler_params=pltpu.CompilerParams(dimension_semantics=("arbitrary",)),
         cost_estimate=cost,
-    )(scal, dtab, q, keys, values, m, l, acc)
+    )(scal, dtab, q, pairs, pairs, m, l, acc)
 
 
 def rms_scale(rows, gain):
@@ -187,35 +190,33 @@
     )
     own_tiles = fresh_keys.shape[0] // KEY_TILE
     no_skip = (0, 0)
+    own_pairs = jnp.concatenate([fresh_keys, fresh_values], 1)
     state = attend(
         state,
         rows_q,
-        fresh_keys,
-        fresh_values,
+        own_pairs,
         (0, (partner - seq_index) * tok_rows),
         own_tiles,
         no_skip,
         dtab,
     )
-    prior_k = lax.all_gather(cached_keys, "seq", axis=0, tiled=True)
-    prior_v = lax.all_gather(cached_values, "seq", axis=0, tiled=True)
+    prior_pairs = lax.all_gather(
+        jnp.concatenate([cached_keys, cached_values], 1), "seq", axis=0, tiled=True
+    )
     state = attend(
         state,
         rows_q,
-        prior_k,
-        prior_v,
+        prior_pairs,
         (offset + seq_index * tok_rows, offset + partner * tok_rows),
-        prior_k.shape[0] // KEY_TILE,
+        prior_pairs.shape[0] // KEY_TILE,
         no_skip,
         dtab,
     )
-    all_k = lax.all_gather(fresh_keys, "seq", axis=0, tiled=True)
-    all_v = lax.all_gather(fresh_values, "seq", axis=0, tiled=True)
+    all_pairs = lax.all_gather(own_pairs, "seq", axis=0, tiled=True)
     state = attend(
         state,
         rows_q,
-        all_k,
-        all_v,
+        all_pairs,
         (seq_index * tok_rows, partner * tok_rows),
         jnp.maximum(seq_index * own_tiles + own_tiles // 2, (partner + 1) * own_tiles),
         (seq_index * own_tiles, (seq_index + 1) * own_tiles),

time: 618 us -> 577 us (0.934)
  waiting for transfers between devices: 167 us -> 124 us
    all_gather x4 -> x2, waiting for transfers between devices: 70.8 us -> 30.1 us  [the longest x1 30.1 us: per_device(): lax.all_gather(jnp.concatenate([cached_keys, cached_values], 1), 'seq', a...]
  transfers between devices with their start and end apart: 9 -> 7, of which waited for: 5 -> 4; matrix products, arithmetic and copies ran while one was open for 4% -> 5% of each run, Pallas kernels for 47% -> 50%
where the time goes in v2:
time: 577 us
  Pallas kernels  290 us (50%)
  waiting for transfers between devices  124 us (21%)
  local copies, waits for them, and re-layouts  71.7 us (12%)
  matrix products  34.3 us (6%)
  other arithmetic  29.2 us (5%)
  between operations  14.4 us (2%)
  starting transfers between devices  13.2 us (2%)
    pallas_call x3, Pallas kernels, attend(): pl.pallas_call(attn_kernel, out_shape=(jax.ShapeDtypeStruct(m.shape, jnp....  290 us
    reduce_scatter x1, waiting for transfers between devices, per_device(): lax.psum_scatter(combined.astype(jnp.bfloat16), 'tensor', scatter_dimensi...  56.2 us
    all_gather x1, waiting for transfers between devices, per_device(): attended_full = lax.all_gather(attended, 'tensor', axis=1, tiled=True)  33.5 us
    all_gather x1, waiting for transfers between devices, per_device(): lax.all_gather(jnp.concatenate([cached_keys, cached_values], 1), 'seq', a...  30.1 us
    gather x2, local copies, waits for them, and re-layouts, per_device(): picked = jnp.take(expert_rows, target, axis=0).reshape(tok_rows, TOP, D)  26.8 us
    reduce_sum x1, other arithmetic, per_device(): combined = jnp.sum(picked * route_weights[:, :, None], axis=1)  17.5 us
    dot_general x1, matrix products, per_device(): jnp.einsum('ecd,edgf->ecgf', buffer, expert_in, preferred_element_type=jn...  15.6 us
    gather x1, local copies, waits for them, and re-layouts, per_device(): buffer = jnp.take(normed, slot_owner, axis=0).reshape(expert_count, CAP, D)  14 us
  transfers between devices with their start and end apart: 7, of which 4 were waited for; matrix products, arithmetic and copies ran while one was open for 5% of the time, Pallas kernels for 50%

profile of v2, /device:TPU:1, one launch (start us, length us, event | category | flops | bytes accessed | tf_op | source)
XLA Modules:
  0.0 576.7 jit_solution(1166010920251317882)
XLA Ops:
  6.5 1.8 pad_maximum_fusion
  8.4 1.0 constant_dynamic-update-slice_fusion.1
  9.4 1.0 constant_dynamic-update-slice_fusion.k_ref.v_ref
  10.5 0.8 copy-done.2
  11.3 1.0 fusion.38
  12.3 7.7 %collective-permute-start = (bf16[512,128]{1,0:T(8,128)(2,1)S(1)}, bf16[512,128]{1,0:T(8,128)(2,1)S(1)}, u32[]{:S(2)}, u32[]{:S(2)}) collective-permute-start(bf16[512,128]{1,0:T(8,128)(2,1)S(1)} %get-tuple-element.24), channel_id=1, source_target_pairs={{0,120},{8,112},{16,104},{24,96},{32,88},{40,80},{48,72},{56,64},{... | collective-permute-start | bytes 393224 | tf_op jit(solution)/shard_map/ppermute | solution.py:184
  20.1 0.8 copy.42
  20.8 0.9 slice_reduce_fusion.1
  21.7 0.6 broadcast_subtract_fusion.dtab_ref
  23.0 0.7 stack.38.scal_ref
  23.6 0.6 pad_add_fusion
  24.3 0.7 pad_maximum_fusion.1.q_ref
  25.0 1.0 broadcast_in_dim.49.m_in
  26.0 1.1 broadcast_in_dim.50.l_in
  27.1 0.8 broadcast_in_dim.51.acc_in
  27.9 19.3 %shard_map.136 = (f32[2,1024,128]{2,1,0:T(8,128)}, f32[2,1024,128]{2,1,0:T(8,128)}, f32[1024,128]{1,0:T(8,128)}) custom-call(s32[5]{0:T(128)} %get-tuple-element.25.scal_ref, f32[32,2]{1,0:T(8,128)} %broadcast_subtract_fusion.dtab_ref, bf16[1024,128]{1,0:T(8,128)(2,1)} %pad_maximum_fusion.1.q_ref, bf16[1024,256]{1,0:T(8,128)(2,1)} %copy-done.2, ...), custom_call_target="tpu_custom_call" | custom-call | flops 2147483648 | bytes 3670016 | tf_op jit(solution)/shard_map/pallas_call | solution.py:124
  47.3 30.1 %all-gather.7.cloned.1.call-done.k_ref.v_ref = bf16[12288,256]{1,0:T(8,128)(2,1)} async-done(((bf16[768,256]{1,0:T(8,128)(2,1)}), bf16[12288,256]{1,0:T(8,128)(2,1)}) %all-gather.7.cloned.1.call-update) | async-done | bytes 6291472 | tf_op jit(solution)/shard_map/all_gather | solution.py:203
  77.3 153.8 %shard_map.137 = (f32[2,1024,128]{2,1,0:T(8,128)}, f32[2,1024,128]{2,1,0:T(8,128)}, f32[1024,128]{1,0:T(8,128)}) custom-call(s32[5]{0:T(128)} %get-tuple-element.26.scal_ref, f32[32,2]{1,0:T(8,128)} %broadcast_subtract_fusion.dtab_ref, bf16[1024,128]{1,0:T(8,128)(2,1)} %pad_maximum_fusion.1.q_ref, ...), custom_call_target="tpu_custom_call" | custom-call | flops 25769803776 | bytes 9437184 | tf_op jit(solution)/shard_map/pallas_call | solution.py:124
  231.1 117.1 %shard_map.138 = (f32[2,1024,128]{2,1,0:T(8,128)}, f32[2,1024,128]{2,1,0:T(8,128)}, f32[1024,128]{1,0:T(8,128)}) custom-call(s32[5]{0:T(128)} %stack.38.scal_ref, f32[32,2]{1,0:T(8,128)} %broadcast_subtract_fusion.dtab_ref, bf16[1024,128]{1,0:T(8,128)(2,1)} %pad_maximum_fusion.1.q_ref, bf16[16384,256]{1,0:T(8,128)(2,1)} %all-gather.5.cloned.1.call-done.k_ref.v_ref, ...), custom_call_target="tpu_custom_call" | custom-call | flops 34359738368 | bytes 11534336 | tf_op jit(solution)/shard_map/pallas_call | solution.py:124
  348.2 1.6 fusion.21
  349.9 5.3 collective-permute-start.1
  355.2 3.9 collective-permute-done.1
  359.0 0.7 pad_maximum_fusion.2
  360.1 0.3 eq.26
  360.4 0.3 reshape.92
  360.6 2.6 copy.41
  363.2 2.3 reduce-window.6
  365.5 0.3 slice_reduce_fusion
  366.0 0.2 copy.47
  366.2 0.3 mul.107
  366.7 0.5 reduce_sum.32
  367.2 8.1 %scatter_custom_fusion = s32[3072]{0:T(1024)S(1)} fusion(s32[2048]{0:T(1024)S(1)} %bitcast.66, s32[2048]{0:T(1024)S(1)} %add_select_fusion, s32[]{:T(128)} %constant.47.clone.1), kind=kCustom, calls=%fused_computation.59 | custom fusion | bytes 12292 | tf_op jit(solution)/shard_map/scatter | solution.py:248
  375.5 0.3 copy.46
  376.1 33.5 %all-gather.9.cloned.1.call-done = bf16[1024,1024]{1,0:T(8,128)(2,1)} async-done(((bf16[1024,128]{1,0:T(8,128)(2,1)}), bf16[1024,1024]{1,0:T(8,128)(2,1)}) %all-gather.9.cloned.1.call-update) | async-done | bytes 2097168 | tf_op jit(solution)/shard_map/all_gather | solution.py:230
  409.6 5.4 multiply_reduce_fusion.1
  415.1 2.0 copy-done
  417.0 1.7 multiply_convert_fusion
  418.8 3.0 copy.48
  421.8 14.0 %gather_fusion = bf16[3072,1024]{1,0:T(8,128)(2,1)} fusion(bf16[1024,1024]{1,0:T(8,128)(2,1)S(1)} %copy.48, s32[3072]{0:T(1024)S(1)} %fusion.26), kind=kCustom, calls=%fused_computation | custom fusion | bytes 12595200 | tf_op jit(solution)/shard_map/jit(_take)/gather | solution.py:249
  435.7 15.6 %fusion = f32[8,384,2,352]{1,3,2,0:T(8,128)} fusion(bf16[8,1024,2,352]{1,3,2,0:T(8,128)(2,1)} %param.26, bf16[8,384,1024]{2,1,0:T(8,128)(2,1)} %bitcast.64, pred[8,384]{1,0:T(8,128)(4,1)S(1)} %broadcast_in_dim.55), kind=kOutput, calls=%fused_computation.5 | convolution fusion | flops 4432330752 | bytes 26479616 | tf_op jit(solution)/shard_map/ecd,edgf->ecgf/dot_general | solution.py:250
  451.3 13.3 %fusion.14 = f32[8,384,1024]{2,1,0:T(8,128)} fusion(bf16[8,352,1024]{2,1,0:T(8,128)(2,1)} %param.27, f32[8,384,2,352]{1,3,2,0:T(8,128)} %fusion), kind=kOutput, calls=%fused_computation.24 | convolution fusion | flops 2225405952 | bytes 27000832 | tf_op jit(solution)/shard_map/ecf,efd->ecd/dot_general | solution.py:254
  464.6 16.3 %gather_fusion.1 = f32[2048,1024]{1,0:T(8,128)} fusion(f32[3072,1024]{1,0:T(8,128)} %bitcast.63, s32[2048]{0:T(1024)S(1)} %broadcast_clamp_fusion), kind=kCustom, calls=%fused_computation.1 | custom fusion | bytes 16785408 | tf_op jit(solution)/shard_map/jit(_take)/gather | solution.py:257
  480.9 10.6 %gather.15 = f32[1024,2,1024]{2,1,0:T(2,128)} reshape(f32[2048,1024]{1,0:T(8,128)} %gather_fusion.1) | data formatting | bytes 16777216 | tf_op jit(solution)/shard_map/jit(_take)/gather | solution.py:257
  491.4 17.5 %multiply_reduce_fusion = bf16[1024,1024]{1,0:T(8,128)(2,1)S(1)} fusion(f32[1024,2,1024]{2,1,0:T(2,128)} %gather.15, pred[1024,2]{1,0:T(8,128)(4,1)S(1)} %copy.46, f32[1024,2]{1,0:T(8,128)S(1)} %copy.50), kind=kLoop, calls=%fused_computation.3 | loop fusion | flops 5242880 | bytes 10496000 | tf_op jit(solution)/shard_map/reduce_sum | solution.py:258
  509.0 2.6 copy.51
  511.6 56.2 %reduce-scatter.2.cloned.1.call-done = bf16[1024,128]{0,1:T(8,128)(2,1)} async-done(((bf16[1024,1024]{0,1:T(8,128)(2,1)}), bf16[1024,128]{0,1:T(8,128)(2,1)}) %reduce-scatter.2.cloned.1.call-update) | async-done | bytes 262160 | tf_op jit(solution)/shard_map/reduce_scatter | solution.py:259
  567.8 1.2 add_convert_fusion
  569.0 0.8 copy.52
  (42 shorter events, 1.3 us)
Async XLA Ops:
  6.5 70.8 %all-gather.7.cloned.1.call-start = ((), (), s32[]{:S(2)}) async-start(), calls=%async_computation.2 | async-start | bytes 6684672 | tf_op jit(solution)/shard_map/all_gather | solution.py:203
  8.4 222.7 %all-gather.5.cloned.1.call-start = ((), (), s32[]{:S(2)}) async-start(), calls=%async_computation.1 | async-start | bytes 8912896 | tf_op jit(solution)/shard_map/all_gather | solution.py:215
  10.5 0.8 copy-start.2
  11.3 364.8 %all-gather.11.cloned.1.call-start = ((), (), s32[]{:S(2)}) async-start(), calls=%async_computation.4 | async-start | bytes 2359296 | tf_op jit(solution)/shard_map/all_gather | solution.py:231
  12.3 11.9 %collective-permute-start = (bf16[512,128]{1,0:T(8,128)(2,1)S(1)}, bf16[512,128]{1,0:T(8,128)(2,1)S(1)}, u32[]{:S(2)}, u32[]{:S(2)}) collective-permute-start(bf16[512,128]{1,0:T(8,128)(2,1)S(1)} %get-tuple-element.24), channel_id=1, source_target_pairs={{0,120},{8,112},{16,104},{24,96},{32,88},{40,80},{48,72},{56,64},{... | collective-permute-start | bytes 393224 | tf_op jit(solution)/shard_map/ppermute | solution.py:184
  20.0 389.5 %all-gather.9.cloned.1.call-start = ((), (), s32[]{:S(2)}) async-start(), calls=%async_computation.3 | async-start | bytes 2359296 | tf_op jit(solution)/shard_map/all_gather | solution.py:230
  231.1 128.8 %copy-start.3 = (s32[1024,2]{0,1:T(2,128)S(1)}, s32[1024,2]{0,1:T(2,128)}, u32[]{:S(2)}) copy-start(s32[1024,2]{0,1:T(2,128)} %param.24) | copy-start | bytes 24580
  348.2 12.4 %copy-start.1 = (bf16[1024,1024]{1,0:T(8,128)(2,1)S(1)}, bf16[1024,1024]{1,0:T(8,128)(2,1)}, u32[]{:S(2)}) copy-start(bf16[1024,1024]{1,0:T(8,128)(2,1)} %param.14) | copy-start | bytes 6291460
  349.9 9.2 %collective-permute-start.1 = (bf16[512,128]{1,0:T(8,128)(2,1)S(1)}, bf16[512,128]{1,0:T(8,128)(2,1)S(1)}, u32[]{:S(2)}, u32[]{:S(2)}) collective-permute-start(bf16[512,128]{1,0:T(8,128)(2,1)S(1)} %get-tuple-element.22), channel_id=1, source_target_pairs={{0,120},{8,112},{16,104},{24,96},{32,88},{40,80},{48,72},{56,64},{... | collective-permute-start | bytes 393224 | tf_op jit(solution)/shard_map/ppermute | solution.py:229
  359.8 16.0 %copy-start.4 = (f32[1024,2]{0,1:T(2,128)S(1)}, f32[1024,2]{0,1:T(2,128)}, u32[]{:S(2)}) copy-start(f32[1024,2]{0,1:T(2,128)} %param.25) | copy-start | bytes 24580
  359.8 208.0 %reduce-scatter.2.cloned.1.call-start = ((), (), s32[]{:S(2)}) async-start(), calls=%async_computation.5 | async-start | bytes 2359296 | tf_op jit(solution)/shard_map/reduce_scatter | solution.py:259
  376.0 41.0 %copy-start.5 = (f32[1024]{0:T(1024)S(1)}, f32[1024]{0:T(1024)}, u32[]{:S(2)}) copy-start(f32[1024]{0:T(1024)} %param.23) | copy-start | bytes 12292
  415.0 2.0 copy-start
Sparse Core Ops, SparseCore 0:
  9.8 67.4 all-gather.6
  79.8 70.6 all-gather.4
  152.1 48.6 all-gather.10
  359.9 49.6 all-gather.8
  511.7 56.0 reduce-scatter.1

commit v3 on v2

--- a/solution.py
+++ b/solution.py
@@ -182,6 +182,17 @@
     partner = n_seq - 1 - seq_index
     swap = [(i, n_seq - 1 - i) for i in range(n_seq)]
     rows_q = jnp.concatenate([queries[:half], lax.ppermute(queries[half:], "seq", swap)], 0)
+    expert_count = expert_in.shape[0]
+    flat_routes = routes.reshape(-1)
+    onehot = (flat_routes[:, None] == jnp.arange(expert_count, dtype=jnp.int32)[None, :]).astype(
+        jnp.int32
+    )
+    before = jnp.cumsum(onehot, axis=0) - onehot
+    slot = jnp.sum(before * onehot, axis=1)
+    target = flat_routes * CAP + slot
+    owner = jnp.arange(flat_routes.shape[0], dtype=jnp.int32) // TOP
+    slot_owner = jnp.zeros((expert_count * CAP,), jnp.int32).at[target].set(owner)
+    slot_owner, target, rows_q = lax.optimization_barrier((slot_owner, target, rows_q))
     dtab = bias_table - bias_table[bias_table.shape[0] - 1][None, :]
     state = (
         jnp.full((2, tok_rows, 128), lowest, jnp.float32),
@@ -236,16 +247,6 @@
     )
     normed = rms_scale(resid, norm_gain)
     resid_cols = lax.dynamic_slice_in_dim(resid, col_start, col_width, 1)
-    expert_count = expert_in.shape[0]
-    flat_routes = routes.reshape(-1)
-    onehot = (flat_routes[:, None] == jnp.arange(expert_count, dtype=jnp.int32)[None, :]).astype(
-        jnp.int32
-    )
-    before = jnp.cumsum(onehot, axis=0) - onehot
-    slot = jnp.sum(before * onehot, axis=1)
-    target = flat_routes * CAP + slot
-    owner = jnp.arange(flat_routes.shape[0], dtype=jnp.int32) // TOP
-    slot_owner = jnp.zeros((expert_count * CAP,), jnp.int32).at[target].set(owner)
     buffer = jnp.take(normed, slot_owner, axis=0).reshape(expert_count, CAP, D)
     gate_up = jnp.einsum("ecd,edgf->ecgf", buffer, expert_in, preferred_element_type=jnp.float32)
     hidden = (jax.nn.gelu(gate_up[:, :, 0], approximate=True) * gate_up[:, :, 1]).astype(

time: 577 us -> 580 us (level)
  Pallas kernels: 290 us -> 305 us
  waiting for transfers between devices: 124 us -> 110 us
    all_gather x1, waiting for transfers between devices: 30.1 us -> 3.49 us  [per_device(): lax.all_gather(jnp.concatenate([cached_keys, cached_values], 1), 'seq', a...]
    pallas_call x3, Pallas kernels: 290 us -> 305 us  [attend(): pl.pallas_call(attn_kernel, out_shape=(jax.ShapeDtypeStruct(m.shape, jnp....]
    all_gather x1, waiting for transfers between devices: 33.5 us -> 46.3 us  [per_device(): attended_full = lax.all_gather(attended, 'tensor', axis=1, tiled=True)]
  transfers between devices with their start and end apart: 7 -> 7, of which waited for: 4 -> 4; matrix products, arithmetic and copies ran while one was open for 5% -> 5% of each run, Pallas kernels for 50% -> 53%
where the time goes in v3:
time: 580 us; the launch traced here: 576 us
  Pallas kernels  305 us (53%)
  waiting for transfers between devices  110 us (19%)
  local copies, waits for them, and re-layouts  70.5 us (12%)
  matrix products  34.3 us (6%)
  other arithmetic  29 us (5%)
  between operations  14.3 us (2%)
  starting transfers between devices  13.2 us (2%)
    pallas_call x3, Pallas kernels, attend(): pl.pallas_call(attn_kernel, out_shape=(jax.ShapeDtypeStruct(m.shape, jnp....  305 us
    reduce_scatter x1, waiting for transfers between devices, per_device(): lax.psum_scatter(combined.astype(jnp.bfloat16), 'tensor', scatter_dimensi...  56.2 us
    all_gather x1, waiting for transfers between devices, per_device(): attended_full = lax.all_gather(attended, 'tensor', axis=1, tiled=True)  46.3 us
    gather x2, local copies, waits for them, and re-layouts, per_device(): picked = jnp.take(expert_rows, target, axis=0).reshape(tok_rows, TOP, D)  26.8 us
    reduce_sum x1, other arithmetic, per_device(): combined = jnp.sum(picked * route_weights[:, :, None], axis=1)  17.3 us
    dot_general x1, matrix products, per_device(): jnp.einsum('ecd,edgf->ecgf', buffer, expert_in, preferred_element_type=jn...  15.6 us
    gather x1, local copies, waits for them, and re-layouts, per_device(): buffer = jnp.take(normed, slot_owner, axis=0).reshape(expert_count, CAP, D)  14 us
    dot_general x1, matrix products, per_device(): jnp.einsum('ecf,efd->ecd', hidden, expert_out, preferred_element_type=jnp...  13.3 us
  transfers between devices with their start and end apart: 7, of which 4 were waited for; matrix products, arithmetic and copies ran while one was open for 5% of the time, Pallas kernels for 53%

profile of v3, /device:TPU:1, one launch (start us, length us, event | category | flops | bytes accessed | tf_op | source)
XLA Modules:
  0.0 576.1 jit_solution(5575367181593480425)
XLA Ops:
  6.5 1.8 pad_maximum_fusion
  8.5 1.0 constant_dynamic-update-slice_fusion.1
  9.5 1.0 constant_dynamic-update-slice_fusion.k_ref.v_ref
  10.5 0.8 copy-done.2
  11.4 1.0 fusion.39
  12.3 7.7 %collective-permute-start = (bf16[512,128]{1,0:T(8,128)(2,1)S(1)}, bf16[512,128]{1,0:T(8,128)(2,1)S(1)}, u32[]{:S(2)}, u32[]{:S(2)}) collective-permute-start(bf16[512,128]{1,0:T(8,128)(2,1)S(1)} %get-tuple-element.30), channel_id=1, source_target_pairs={{0,120},{8,112},{16,104},{24,96},{32,88},{40,80},{48,72},{56,64},{... | collective-permute-start | bytes 393224 | tf_op jit(solution)/shard_map/ppermute | solution.py:184
  20.1 0.9 copy.33
  21.0 0.3 eq.29
  21.3 0.3 eq.25
  21.7 0.2 slice_reduce_fusion.1
  21.9 2.3 reduce-window.6
  24.2 0.3 slice_reduce_fusion
  24.8 0.2 copy.32
  25.0 0.3 mul.105
  25.4 0.6 broadcast_subtract_fusion.dtab_ref
  26.6 8.1 %scatter_custom_fusion = s32[3072]{0:T(1024)S(1)} fusion(s32[2048]{0:T(1024)S(1)} %bitcast.67, s32[2048]{0:T(1024)S(1)} %add_select_fusion, s32[]{:T(128)} %constant.46.clone.1), kind=kCustom, calls=%fused_computation.61 | custom fusion | bytes 12292 | tf_op jit(solution)/shard_map/scatter | solution.py:194
  34.7 0.6 stack.38.scal_ref
  35.3 0.6 pad_add_fusion
  35.9 0.7 pad_maximum_fusion.1.q_ref
  36.7 1.0 broadcast_in_dim.54.m_in
  37.7 1.1 broadcast_in_dim.55.l_in
  38.8 0.8 broadcast_in_dim.56.acc_in
  39.6 34.2 %shard_map.136 = (f32[2,1024,128]{2,1,0:T(8,128)}, f32[2,1024,128]{2,1,0:T(8,128)}, f32[1024,128]{1,0:T(8,128)}) custom-call(s32[5]{0:T(128)} %get-tuple-element.31.scal_ref, f32[32,2]{1,0:T(8,128)} %broadcast_subtract_fusion.dtab_ref, bf16[1024,128]{1,0:T(8,128)(2,1)} %pad_maximum_fusion.1.q_ref, bf16[1024,256]{1,0:T(8,128)(2,1)} %copy-done.2, ...), custom_call_target="tpu_custom_call" | custom-call | flops 2147483648 | bytes 3670016 | tf_op jit(solution)/shard_map/pallas_call | solution.py:124
  73.8 3.5 all-gather.7.cloned.1.call-done.k_ref.v_ref
  77.3 153.7 %shard_map.137 = (f32[2,1024,128]{2,1,0:T(8,128)}, f32[2,1024,128]{2,1,0:T(8,128)}, f32[1024,128]{1,0:T(8,128)}) custom-call(s32[5]{0:T(128)} %get-tuple-element.32.scal_ref, f32[32,2]{1,0:T(8,128)} %broadcast_subtract_fusion.dtab_ref, bf16[1024,128]{1,0:T(8,128)(2,1)} %pad_maximum_fusion.1.q_ref, ...), custom_call_target="tpu_custom_call" | custom-call | flops 25769803776 | bytes 9437184 | tf_op jit(solution)/shard_map/pallas_call | solution.py:124
  231.0 117.0 %shard_map.138 = (f32[2,1024,128]{2,1,0:T(8,128)}, f32[2,1024,128]{2,1,0:T(8,128)}, f32[1024,128]{1,0:T(8,128)}) custom-call(s32[5]{0:T(128)} %stack.38.scal_ref, f32[32,2]{1,0:T(8,128)} %broadcast_subtract_fusion.dtab_ref, bf16[1024,128]{1,0:T(8,128)(2,1)} %pad_maximum_fusion.1.q_ref, bf16[16384,256]{1,0:T(8,128)(2,1)} %all-gather.5.cloned.1.call-done.k_ref.v_ref, ...), custom_call_target="tpu_custom_call" | custom-call | flops 34359738368 | bytes 11534336 | tf_op jit(solution)/shard_map/pallas_call | solution.py:124
  348.1 1.6 fusion.21
  349.7 5.3 collective-permute-start.1
  355.0 3.9 collective-permute-done.1
  358.9 0.7 pad_maximum_fusion.2
  359.7 2.6 copy.30
  362.3 0.2 copy.37
  362.5 0.5 broadcast_in_dim.58
  363.2 46.3 %all-gather.9.cloned.1.call-done = bf16[1024,1024]{1,0:T(8,128)(2,1)} async-done(((bf16[1024,128]{1,0:T(8,128)(2,1)}), bf16[1024,1024]{1,0:T(8,128)(2,1)}) %all-gather.9.cloned.1.call-update) | async-done | bytes 2097168 | tf_op jit(solution)/shard_map/all_gather | solution.py:241
  409.4 5.4 multiply_reduce_fusion.1
  414.9 2.0 copy-done
  416.9 1.8 multiply_convert_fusion
  418.6 2.9 copy.35
  421.5 14.0 %gather_fusion = bf16[3072,1024]{1,0:T(8,128)(2,1)} fusion(bf16[1024,1024]{1,0:T(8,128)(2,1)S(1)} %copy.35, s32[3072]{0:T(1024)S(1)} %fusion.26), kind=kCustom, calls=%fused_computation | custom fusion | bytes 12595200 | tf_op jit(solution)/shard_map/jit(_take)/gather | solution.py:250
  435.5 15.6 %fusion = f32[8,384,2,352]{1,3,2,0:T(8,128)} fusion(bf16[8,1024,2,352]{1,3,2,0:T(8,128)(2,1)} %param.26, bf16[8,384,1024]{2,1,0:T(8,128)(2,1)} %bitcast.64, pred[8,384]{1,0:T(8,128)(4,1)S(1)} %broadcast_in_dim.60), kind=kOutput, calls=%fused_computation.5 | convolution fusion | flops 4432330752 | bytes 26479616 | tf_op jit(solution)/shard_map/ecd,edgf->ecgf/dot_general | solution.py:251
  451.1 13.3 %fusion.14 = f32[8,384,1024]{2,1,0:T(8,128)} fusion(bf16[8,352,1024]{2,1,0:T(8,128)(2,1)} %param.27, f32[8,384,2,352]{1,3,2,0:T(8,128)} %fusion), kind=kOutput, calls=%fused_computation.24 | convolution fusion | flops 2225405952 | bytes 27000832 | tf_op jit(solution)/shard_map/ecf,efd->ecd/dot_general | solution.py:255
  464.4 16.2 %gather_fusion.1 = f32[2048,1024]{1,0:T(8,128)} fusion(f32[3072,1024]{1,0:T(8,128)} %bitcast.63, s32[2048]{0:T(1024)S(1)} %fusion.30), kind=kCustom, calls=%fused_computation.1 | custom fusion | bytes 16785408 | tf_op jit(solution)/shard_map/jit(_take)/gather | solution.py:258
  480.6 10.6 %gather.15 = f32[1024,2,1024]{2,1,0:T(2,128)} reshape(f32[2048,1024]{1,0:T(8,128)} %gather_fusion.1) | data formatting | bytes 16777216 | tf_op jit(solution)/shard_map/jit(_take)/gather | solution.py:258
  491.2 17.3 %multiply_reduce_fusion = bf16[1024,1024]{1,0:T(8,128)(2,1)S(1)} fusion(f32[1024,2,1024]{2,1,0:T(2,128)} %gather.15, pred[1024,2]{1,0:T(8,128)(4,1)S(1)} %broadcast_in_dim.58, f32[1024,2]{1,0:T(8,128)S(1)} %copy.37), kind=kLoop, calls=%fused_computation.3 | loop fusion | flops 5242880 | bytes 10496000 | tf_op jit(solution)/shard_map/reduce_sum | solution.py:259
  508.5 2.6 copy.38
  511.1 56.2 %reduce-scatter.2.cloned.1.call-done = bf16[1024,128]{0,1:T(8,128)(2,1)} async-done(((bf16[1024,1024]{0,1:T(8,128)(2,1)}), bf16[1024,128]{0,1:T(8,128)(2,1)}) %reduce-scatter.2.cloned.1.call-update) | async-done | bytes 262160 | tf_op jit(solution)/shard_map/reduce_scatter | solution.py:260
  567.4 1.2 add_convert_fusion
  568.6 0.8 copy.39
  (43 shorter events, 0.8 us)
Async XLA Ops:
  6.5 15.0 %copy-start.3 = (s32[1024,2]{0,1:T(2,128)S(1)}, s32[1024,2]{0,1:T(2,128)}, u32[]{:S(2)}) copy-start(s32[1024,2]{0,1:T(2,128)} %param.24) | copy-start | bytes 24580
  6.5 15.1 %copy-start.6 = (f32[32,2]{0,1:T(2,128)S(1)}, f32[32,2]{0,1:T(2,128)}, u32[]{:S(2)}) copy-start(f32[32,2]{0,1:T(2,128)} %param.21) | copy-start | bytes 772
  6.5 70.8 %all-gather.7.cloned.1.call-start = ((), (), s32[]{:S(2)}) async-start(), calls=%async_computation.2 | async-start | bytes 6684672 | tf_op jit(solution)/shard_map/all_gather | solution.py:214
  8.4 222.6 %all-gather.5.cloned.1.call-start = ((), (), s32[]{:S(2)}) async-start(), calls=%async_computation.1 | async-start | bytes 8912896 | tf_op jit(solution)/shard_map/all_gather | solution.py:226
  10.5 0.8 copy-start.2
  11.3 351.9 %all-gather.11.cloned.1.call-start = ((), (), s32[]{:S(2)}) async-start(), calls=%async_computation.4 | async-start | bytes 2359296 | tf_op jit(solution)/shard_map/all_gather | solution.py:242
  12.3 23.6 %collective-permute-start = (bf16[512,128]{1,0:T(8,128)(2,1)S(1)}, bf16[512,128]{1,0:T(8,128)(2,1)S(1)}, u32[]{:S(2)}, u32[]{:S(2)}) collective-permute-start(bf16[512,128]{1,0:T(8,128)(2,1)S(1)} %get-tuple-element.30), channel_id=1, source_target_pairs={{0,120},{8,112},{16,104},{24,96},{32,88},{40,80},{48,72},{56,64},{... | collective-permute-start | bytes 393224 | tf_op jit(solution)/shard_map/ppermute | solution.py:184
  20.0 389.4 %all-gather.9.cloned.1.call-start = ((), (), s32[]{:S(2)}) async-start(), calls=%async_computation.3 | async-start | bytes 2359296 | tf_op jit(solution)/shard_map/all_gather | solution.py:241
  348.1 11.6 %copy-start.1 = (bf16[1024,1024]{1,0:T(8,128)(2,1)S(1)}, bf16[1024,1024]{1,0:T(8,128)(2,1)}, u32[]{:S(2)}) copy-start(bf16[1024,1024]{1,0:T(8,128)(2,1)} %param.14) | copy-start | bytes 6291460
  348.1 14.2 %copy-start.4 = (f32[1024,2]{0,1:T(2,128)S(1)}, f32[1024,2]{0,1:T(2,128)}, u32[]{:S(2)}) copy-start(f32[1024,2]{0,1:T(2,128)} %param.25) | copy-start | bytes 24580
  349.7 9.2 %collective-permute-start.1 = (bf16[512,128]{1,0:T(8,128)(2,1)S(1)}, bf16[512,128]{1,0:T(8,128)(2,1)S(1)}, u32[]{:S(2)}, u32[]{:S(2)}) collective-permute-start(bf16[512,128]{1,0:T(8,128)(2,1)S(1)} %get-tuple-element.28), channel_id=1, source_target_pairs={{0,120},{8,112},{16,104},{24,96},{32,88},{40,80},{48,72},{56,64},{... | collective-permute-start | bytes 393224 | tf_op jit(solution)/shard_map/ppermute | solution.py:240
  359.6 207.8 %reduce-scatter.2.cloned.1.call-start = ((), (), s32[]{:S(2)}) async-start(), calls=%async_computation.5 | async-start | bytes 2359296 | tf_op jit(solution)/shard_map/reduce_scatter | solution.py:260
  363.1 53.8 %copy-start.5 = (f32[1024]{0:T(1024)S(1)}, f32[1024]{0:T(1024)}, u32[]{:S(2)}) copy-start(f32[1024]{0:T(1024)} %param.23) | copy-start | bytes 12292
  414.9 2.0 copy-start
Sparse Core Ops, SparseCore 0:
  9.8 67.4 all-gather.6
  79.8 70.5 all-gather.4
  152.0 48.7 all-gather.10
  359.7 49.6 all-gather.8
  511.3 56.0 reduce-scatter.1

commit v4 on v2

--- a/solution.py
+++ b/solution.py
@@ -39,7 +39,7 @@
     half_blocks = rows_all // ROW_BLOCK // 2
 
     def update(r, near, qk_off):
-        rows = pl.ds(r * ROW_BLOCK, ROW_BLOCK)
+        rows = pl.ds(pl.multiple_of(r * ROW_BLOCK, ROW_BLOCK), ROW_BLOCK)
         q = q_ref[rows, :]
         k = k_ref[...]
         v = v_ref[...]
@@ -85,8 +85,8 @@
 
     @pl.when(active)
     def _():
-        for r in range(rows_all // ROW_BLOCK):
-            qk_off = scal_ref[0] if r < half_blocks else scal_ref[1]
+        def one_block(r, carry):
+            qk_off = jnp.where(r < half_blocks, scal_ref[0], scal_ref[1])
             dmin = qk_off + r * ROW_BLOCK - (t * tk + tk - 1)
             dmax = qk_off + r * ROW_BLOCK + ROW_BLOCK - 1 - t * tk
 
@@ -97,6 +97,10 @@
             @pl.when((dmin < far_edge) & (dmax >= 0))
             def _():
                 update(r, True, qk_off)
+
+            return carry
+
+        lax.fori_loop(0, rows_all // ROW_BLOCK, one_block, 0)
 
 
 def attend(state, q, pairs, offsets, n_valid, skip, dtab):

time: 577 us -> 552 us (0.957)
  Pallas kernels: 290 us -> 265 us
    pallas_call x3, Pallas kernels: 290 us -> 265 us  [attend(): pl.pallas_call(attn_kernel, out_shape=(jax.ShapeDtypeStruct(m.shape, jnp....]
  transfers between devices with their start and end apart: 7 -> 7, of which waited for: 4 -> 4; matrix products, arithmetic and copies ran while one was open for 5% -> 5% of each run, Pallas kernels for 50% -> 48%
where the time goes in v4:
time: 552 us; the launch traced here: 551 us
  Pallas kernels  265 us (48%)
  waiting for transfers between devices  124 us (22%)
  local copies, waits for them, and re-layouts  71.5 us (13%)
  matrix products  34.3 us (6%)
  other arithmetic  29.3 us (5%)
  between operations  14.1 us (3%)
  starting transfers between devices  13.3 us (2%)
    pallas_call x3, Pallas kernels, attend(): pl.pallas_call(attn_kernel, out_shape=(jax.ShapeDtypeStruct(m.shape, jnp....  265 us
    reduce_scatter x1, waiting for transfers between devices, per_device(): lax.psum_scatter(combined.astype(jnp.bfloat16), 'tensor', scatter_dimensi...  56.2 us
    all_gather x1, waiting for transfers between devices, per_device(): attended_full = lax.all_gather(attended, 'tensor', axis=1, tiled=True)  33.2 us
    all_gather x1, waiting for transfers between devices, per_device(): lax.all_gather(jnp.concatenate([cached_keys, cached_values], 1), 'seq', a...  29.9 us
    gather x2, local copies, waits for them, and re-layouts, per_device(): picked = jnp.take(expert_rows, target, axis=0).reshape(tok_rows, TOP, D)  26.8 us
    reduce_sum x1, other arithmetic, per_device(): combined = jnp.sum(picked * route_weights[:, :, None], axis=1)  17.6 us
    dot_general x1, matrix products, per_device(): jnp.einsum('ecd,edgf->ecgf', buffer, expert_in, preferred_element_type=jn...  15.6 us
    gather x1, local copies, waits for them, and re-layouts, per_device(): buffer = jnp.take(normed, slot_owner, axis=0).reshape(expert_count, CAP, D)  14 us
  transfers between devices with their start and end apart: 7, of which 4 were waited for; matrix products, arithmetic and copies ran while one was open for 5% of the time, Pallas kernels for 48%

profile of v4, /device:TPU:1, one launch (start us, length us, event | category | flops | bytes accessed | tf_op | source)
XLA Modules:
  0.0 551.2 jit_solution(15506551287860065746)
XLA Ops:
  6.5 1.8 pad_maximum_fusion
  8.4 1.0 constant_dynamic-update-slice_fusion.1
  9.4 1.0 constant_dynamic-update-slice_fusion.k_ref.v_ref
  10.5 0.8 copy-done.2
  11.3 1.0 fusion.38
  12.3 7.7 %collective-permute-start = (bf16[512,128]{1,0:T(8,128)(2,1)S(1)}, bf16[512,128]{1,0:T(8,128)(2,1)S(1)}, u32[]{:S(2)}, u32[]{:S(2)}) collective-permute-start(bf16[512,128]{1,0:T(8,128)(2,1)S(1)} %get-tuple-element.24), channel_id=1, source_target_pairs={{0,120},{8,112},{16,104},{24,96},{32,88},{40,80},{48,72},{56,64},{... | collective-permute-start | bytes 393224 | tf_op jit(solution)/shard_map/ppermute | solution.py:188
  20.1 0.8 copy.42
  20.8 0.9 slice_reduce_fusion.1
  21.7 0.6 broadcast_subtract_fusion.dtab_ref
  23.0 0.7 stack.38.scal_ref
  23.6 0.6 pad_add_fusion
  24.3 0.7 pad_maximum_fusion.1.q_ref
  25.0 1.0 broadcast_in_dim.49.m_in
  26.0 1.1 broadcast_in_dim.50.l_in
  27.1 0.8 broadcast_in_dim.51.acc_in
  27.9 19.5 %shard_map.136 = (f32[2,1024,128]{2,1,0:T(8,128)}, f32[2,1024,128]{2,1,0:T(8,128)}, f32[1024,128]{1,0:T(8,128)}) custom-call(s32[5]{0:T(128)} %get-tuple-element.25.scal_ref, f32[32,2]{1,0:T(8,128)} %broadcast_subtract_fusion.dtab_ref, bf16[1024,128]{1,0:T(8,128)(2,1)} %pad_maximum_fusion.1.q_ref, bf16[1024,256]{1,0:T(8,128)(2,1)} %copy-done.2, ...), custom_call_target="tpu_custom_call" | custom-call | flops 2147483648 | bytes 3670016 | tf_op jit(solution)/shard_map/pallas_call | solution.py:128
  47.4 29.9 %all-gather.7.cloned.1.call-done.k_ref.v_ref = bf16[12288,256]{1,0:T(8,128)(2,1)} async-done(((bf16[768,256]{1,0:T(8,128)(2,1)}), bf16[12288,256]{1,0:T(8,128)(2,1)}) %all-gather.7.cloned.1.call-update) | async-done | bytes 6291472 | tf_op jit(solution)/shard_map/all_gather | solution.py:207
  77.3 141.5 %shard_map.137 = (f32[2,1024,128]{2,1,0:T(8,128)}, f32[2,1024,128]{2,1,0:T(8,128)}, f32[1024,128]{1,0:T(8,128)}) custom-call(s32[5]{0:T(128)} %get-tuple-element.26.scal_ref, f32[32,2]{1,0:T(8,128)} %broadcast_subtract_fusion.dtab_ref, bf16[1024,128]{1,0:T(8,128)(2,1)} %pad_maximum_fusion.1.q_ref, ...), custom_call_target="tpu_custom_call" | custom-call | flops 25769803776 | bytes 9437184 | tf_op jit(solution)/shard_map/pallas_call | solution.py:128
  218.9 104.3 %shard_map.138 = (f32[2,1024,128]{2,1,0:T(8,128)}, f32[2,1024,128]{2,1,0:T(8,128)}, f32[1024,128]{1,0:T(8,128)}) custom-call(s32[5]{0:T(128)} %stack.38.scal_ref, f32[32,2]{1,0:T(8,128)} %broadcast_subtract_fusion.dtab_ref, bf16[1024,128]{1,0:T(8,128)(2,1)} %pad_maximum_fusion.1.q_ref, bf16[16384,256]{1,0:T(8,128)(2,1)} %all-gather.5.cloned.1.call-done.k_ref.v_ref, ...), custom_call_target="tpu_custom_call" | custom-call | flops 34359738368 | bytes 11534336 | tf_op jit(solution)/shard_map/pallas_call | solution.py:128
  323.1 1.6 fusion.21
  324.7 5.2 collective-permute-start.1
  330.0 4.2 collective-permute-done.1
  334.1 0.7 pad_maximum_fusion.2
  335.4 0.3 eq.26
  335.6 0.3 reshape.92
  335.9 2.6 copy.41
  338.5 2.3 reduce-window.6
  340.8 0.3 slice_reduce_fusion
  341.2 0.2 copy.47
  341.5 0.3 mul.107
  341.9 0.5 reduce_sum.32
  342.4 8.1 %scatter_custom_fusion = s32[3072]{0:T(1024)S(1)} fusion(s32[2048]{0:T(1024)S(1)} %bitcast.66, s32[2048]{0:T(1024)S(1)} %add_select_fusion, s32[]{:T(128)} %constant.47.clone.1), kind=kCustom, calls=%fused_computation.59 | custom fusion | bytes 12292 | tf_op jit(solution)/shard_map/scatter | solution.py:252
  350.8 0.3 copy.46
  351.4 33.2 %all-gather.9.cloned.1.call-done = bf16[1024,1024]{1,0:T(8,128)(2,1)} async-done(((bf16[1024,128]{1,0:T(8,128)(2,1)}), bf16[1024,1024]{1,0:T(8,128)(2,1)}) %all-gather.9.cloned.1.call-update) | async-done | bytes 2097168 | tf_op jit(solution)/shard_map/all_gather | solution.py:234
  384.6 5.4 multiply_reduce_fusion.1
  390.0 2.0 copy-done
  392.0 1.7 multiply_convert_fusion
  393.7 2.9 copy.48
  396.6 14.0 %gather_fusion = bf16[3072,1024]{1,0:T(8,128)(2,1)} fusion(bf16[1024,1024]{1,0:T(8,128)(2,1)S(1)} %copy.48, s32[3072]{0:T(1024)S(1)} %fusion.26), kind=kCustom, calls=%fused_computation | custom fusion | bytes 12595200 | tf_op jit(solution)/shard_map/jit(_take)/gather | solution.py:253
  410.6 15.6 %fusion = f32[8,384,2,352]{1,3,2,0:T(8,128)} fusion(bf16[8,1024,2,352]{1,3,2,0:T(8,128)(2,1)} %param.26, bf16[8,384,1024]{2,1,0:T(8,128)(2,1)} %bitcast.64, pred[8,384]{1,0:T(8,128)(4,1)S(1)} %broadcast_in_dim.55), kind=kOutput, calls=%fused_computation.5 | convolution fusion | flops 4432330752 | bytes 26479616 | tf_op jit(solution)/shard_map/ecd,edgf->ecgf/dot_general | solution.py:254
  426.1 13.3 %fusion.14 = f32[8,384,1024]{2,1,0:T(8,128)} fusion(bf16[8,352,1024]{2,1,0:T(8,128)(2,1)} %param.27, f32[8,384,2,352]{1,3,2,0:T(8,128)} %fusion), kind=kOutput, calls=%fused_computation.24 | convolution fusion | flops 2225405952 | bytes 27000832 | tf_op jit(solution)/shard_map/ecf,efd->ecd/dot_general | solution.py:258
  439.4 16.3 %gather_fusion.1 = f32[2048,1024]{1,0:T(8,128)} fusion(f32[3072,1024]{1,0:T(8,128)} %bitcast.63, s32[2048]{0:T(1024)S(1)} %broadcast_clamp_fusion), kind=kCustom, calls=%fused_computation.1 | custom fusion | bytes 16785408 | tf_op jit(solution)/shard_map/jit(_take)/gather | solution.py:261
  455.7 10.6 %gather.15 = f32[1024,2,1024]{2,1,0:T(2,128)} reshape(f32[2048,1024]{1,0:T(8,128)} %gather_fusion.1) | data formatting | bytes 16777216 | tf_op jit(solution)/shard_map/jit(_take)/gather | solution.py:261
  466.3 17.6 %multiply_reduce_fusion = bf16[1024,1024]{1,0:T(8,128)(2,1)S(1)} fusion(f32[1024,2,1024]{2,1,0:T(2,128)} %gather.15, pred[1024,2]{1,0:T(8,128)(4,1)S(1)} %copy.46, f32[1024,2]{1,0:T(8,128)S(1)} %copy.50), kind=kLoop, calls=%fused_computation.3 | loop fusion | flops 5242880 | bytes 10496000 | tf_op jit(solution)/shard_map/reduce_sum | solution.py:262
  483.9 2.6 copy.51
  486.5 56.2 %reduce-scatter.2.cloned.1.call-done = bf16[1024,128]{0,1:T(8,128)(2,1)} async-done(((bf16[1024,1024]{0,1:T(8,128)(2,1)}), bf16[1024,128]{0,1:T(8,128)(2,1)}) %reduce-scatter.2.cloned.1.call-update) | async-done | bytes 262160 | tf_op jit(solution)/shard_map/reduce_scatter | solution.py:263
  542.7 1.2 add_convert_fusion
  543.8 0.8 copy.52
  (42 shorter events, 1.5 us)
Async XLA Ops:
  6.5 70.8 %all-gather.7.cloned.1.call-start = ((), (), s32[]{:S(2)}) async-start(), calls=%async_computation.2 | async-start | bytes 6684672 | tf_op jit(solution)/shard_map/all_gather | solution.py:207
  8.4 210.5 %all-gather.5.cloned.1.call-start = ((), (), s32[]{:S(2)}) async-start(), calls=%async_computation.1 | async-start | bytes 8912896 | tf_op jit(solution)/shard_map/all_gather | solution.py:219
  10.5 0.8 copy-start.2
  11.3 340.1 %all-gather.11.cloned.1.call-start = ((), (), s32[]{:S(2)}) async-start(), calls=%async_computation.4 | async-start | bytes 2359296 | tf_op jit(solution)/shard_map/all_gather | solution.py:235
  12.3 11.9 %collective-permute-start = (bf16[512,128]{1,0:T(8,128)(2,1)S(1)}, bf16[512,128]{1,0:T(8,128)(2,1)S(1)}, u32[]{:S(2)}, u32[]{:S(2)}) collective-permute-start(bf16[512,128]{1,0:T(8,128)(2,1)S(1)} %get-tuple-element.24), channel_id=1, source_target_pairs={{0,120},{8,112},{16,104},{24,96},{32,88},{40,80},{48,72},{56,64},{... | collective-permute-start | bytes 393224 | tf_op jit(solution)/shard_map/ppermute | solution.py:188
  20.0 364.5 %all-gather.9.cloned.1.call-start = ((), (), s32[]{:S(2)}) async-start(), calls=%async_computation.3 | async-start | bytes 2359296 | tf_op jit(solution)/shard_map/all_gather | solution.py:234
  218.9 116.3 %copy-start.3 = (s32[1024,2]{0,1:T(2,128)S(1)}, s32[1024,2]{0,1:T(2,128)}, u32[]{:S(2)}) copy-start(s32[1024,2]{0,1:T(2,128)} %param.24) | copy-start | bytes 24580
  323.1 12.8 %copy-start.1 = (bf16[1024,1024]{1,0:T(8,128)(2,1)S(1)}, bf16[1024,1024]{1,0:T(8,128)(2,1)}, u32[]{:S(2)}) copy-start(bf16[1024,1024]{1,0:T(8,128)(2,1)} %param.14) | copy-start | bytes 6291460
  324.7 9.4 %collective-permute-start.1 = (bf16[512,128]{1,0:T(8,128)(2,1)S(1)}, bf16[512,128]{1,0:T(8,128)(2,1)S(1)}, u32[]{:S(2)}, u32[]{:S(2)}) collective-permute-start(bf16[512,128]{1,0:T(8,128)(2,1)S(1)} %get-tuple-element.22), channel_id=1, source_target_pairs={{0,120},{8,112},{16,104},{24,96},{32,88},{40,80},{48,72},{56,64},{... | collective-permute-start | bytes 393224 | tf_op jit(solution)/shard_map/ppermute | solution.py:233
  334.9 16.2 %copy-start.4 = (f32[1024,2]{0,1:T(2,128)S(1)}, f32[1024,2]{0,1:T(2,128)}, u32[]{:S(2)}) copy-start(f32[1024,2]{0,1:T(2,128)} %param.25) | copy-start | bytes 24580
  334.9 207.8 %reduce-scatter.2.cloned.1.call-start = ((), (), s32[]{:S(2)}) async-start(), calls=%async_computation.5 | async-start | bytes 2359296 | tf_op jit(solution)/shard_map/reduce_scatter | solution.py:263
  351.3 40.7 %copy-start.5 = (f32[1024]{0:T(1024)S(1)}, f32[1024]{0:T(1024)}, u32[]{:S(2)}) copy-start(f32[1024]{0:T(1024)} %param.23) | copy-start | bytes 12292
  390.0 2.0 copy-start
Sparse Core Ops, SparseCore 0:
  9.8 67.4 all-gather.6
  79.8 70.6 all-gather.4
  152.2 48.4 all-gather.10
  335.0 49.5 all-gather.8
  486.6 56.0 reduce-scatter.1

commit v5 on v4

--- a/solution.py
+++ b/solution.py
@@ -12,7 +12,7 @@
 TOP = 2
 CAP = 384
 KEY_TILE = 512
-ROW_BLOCK = 128
+ROW_BLOCK = 256
 
 
 bucket_edges = [edge for edge in range(1, 17)] + [

time: 552 us -> 466 us (0.84); the launches traced: 551 us -> 457 us
  Pallas kernels: 265 us -> 169 us
    pallas_call x3, Pallas kernels: 265 us -> 169 us  [attend(): pl.pallas_call(attn_kernel, out_shape=(jax.ShapeDtypeStruct(m.shape, jnp....]
  transfers between devices with their start and end apart: 7 -> 7, of which waited for: 4 -> 4; matrix products, arithmetic and copies ran while one was open for 5% -> 6% of each run, Pallas kernels for 48% -> 37%
where the time goes in v5:
time: 466 us; the launch traced here: 457 us
  Pallas kernels  169 us (36%)
  waiting for transfers between devices  127 us (27%)
  local copies, waits for them, and re-layouts  71.7 us (15%)
  matrix products  34.3 us (7%)
  other arithmetic  29.2 us (6%)
  between operations  14.5 us (3%)
  starting transfers between devices  10.5 us (2%)
    pallas_call x3, Pallas kernels, attend(): pl.pallas_call(attn_kernel, out_shape=(jax.ShapeDtypeStruct(m.shape, jnp....  169 us
    reduce_scatter x1, waiting for transfers between devices, per_device(): lax.psum_scatter(combined.astype(jnp.bfloat16), 'tensor', scatter_dimensi...  56.2 us
    all_gather x1, waiting for transfers between devices, per_device(): lax.all_gather(jnp.concatenate([cached_keys, cached_values], 1), 'seq', a...  33.1 us
    all_gather x1, waiting for transfers between devices, per_device(): attended_full = lax.all_gather(attended, 'tensor', axis=1, tiled=True)  31.7 us
    gather x2, local copies, waits for them, and re-layouts, per_device(): picked = jnp.take(expert_rows, target, axis=0).reshape(tok_rows, TOP, D)  26.8 us
    reduce_sum x1, other arithmetic, per_device(): combined = jnp.sum(picked * route_weights[:, :, None], axis=1)  17.6 us
    dot_general x1, matrix products, per_device(): jnp.einsum('ecd,edgf->ecgf', buffer, expert_in, preferred_element_type=jn...  15.6 us
    gather x1, local copies, waits for them, and re-layouts, per_device(): buffer = jnp.take(normed, slot_owner, axis=0).reshape(expert_count, CAP, D)  14 us
  transfers between devices with their start and end apart: 7, of which 4 were waited for; matrix products, arithmetic and copies ran while one was open for 6% of the time, Pallas kernels for 37%

profile of v5, /device:TPU:1, one launch (start us, length us, event | category | flops | bytes accessed | tf_op | source)
XLA Modules:
  0.0 456.9 jit_solution(8695620089453347467)
XLA Ops:
  6.5 1.8 pad_maximum_fusion
  8.4 1.0 constant_dynamic-update-slice_fusion.1
  9.4 1.0 constant_dynamic-update-slice_fusion.k_ref.v_ref
  10.5 0.8 copy-done.2
  11.3 1.0 fusion.38
  12.3 7.7 %collective-permute-start = (bf16[512,128]{1,0:T(8,128)(2,1)S(1)}, bf16[512,128]{1,0:T(8,128)(2,1)S(1)}, u32[]{:S(2)}, u32[]{:S(2)}) collective-permute-start(bf16[512,128]{1,0:T(8,128)(2,1)S(1)} %get-tuple-element.24), channel_id=1, source_target_pairs={{0,120},{8,112},{16,104},{24,96},{32,88},{40,80},{48,72},{56,64},{... | collective-permute-start | bytes 393224 | tf_op jit(solution)/shard_map/ppermute | solution.py:188
  20.1 0.8 copy.42
  20.8 0.9 slice_reduce_fusion.1
  21.7 0.6 broadcast_subtract_fusion.dtab_ref
  23.0 0.7 stack.38.scal_ref
  23.6 0.6 pad_add_fusion
  24.3 0.7 pad_maximum_fusion.1.q_ref
  25.0 1.0 broadcast_in_dim.49.m_in
  26.0 1.1 broadcast_in_dim.50.l_in
  27.1 0.8 broadcast_in_dim.51.acc_in
  27.9 16.2 %shard_map.136 = (f32[2,1024,128]{2,1,0:T(8,128)}, f32[2,1024,128]{2,1,0:T(8,128)}, f32[1024,128]{1,0:T(8,128)}) custom-call(s32[5]{0:T(128)} %get-tuple-element.25.scal_ref, f32[32,2]{1,0:T(8,128)} %broadcast_subtract_fusion.dtab_ref, bf16[1024,128]{1,0:T(8,128)(2,1)} %pad_maximum_fusion.1.q_ref, bf16[1024,256]{1,0:T(8,128)(2,1)} %copy-done.2, ...), custom_call_target="tpu_custom_call" | custom-call | flops 2147483648 | bytes 3670016 | tf_op jit(solution)/shard_map/pallas_call | solution.py:128
  44.2 33.1 %all-gather.7.cloned.1.call-done.k_ref.v_ref = bf16[12288,256]{1,0:T(8,128)(2,1)} async-done(((bf16[768,256]{1,0:T(8,128)(2,1)}), bf16[12288,256]{1,0:T(8,128)(2,1)}) %all-gather.7.cloned.1.call-update) | async-done | bytes 6291472 | tf_op jit(solution)/shard_map/all_gather | solution.py:207
  77.3 82.4 %shard_map.137 = (f32[2,1024,128]{2,1,0:T(8,128)}, f32[2,1024,128]{2,1,0:T(8,128)}, f32[1024,128]{1,0:T(8,128)}) custom-call(s32[5]{0:T(128)} %get-tuple-element.26.scal_ref, f32[32,2]{1,0:T(8,128)} %broadcast_subtract_fusion.dtab_ref, bf16[1024,128]{1,0:T(8,128)(2,1)} %pad_maximum_fusion.1.q_ref, ...), custom_call_target="tpu_custom_call" | custom-call | flops 25769803776 | bytes 9437184 | tf_op jit(solution)/shard_map/pallas_call | solution.py:128
  159.7 70.7 %shard_map.138 = (f32[2,1024,128]{2,1,0:T(8,128)}, f32[2,1024,128]{2,1,0:T(8,128)}, f32[1024,128]{1,0:T(8,128)}) custom-call(s32[5]{0:T(128)} %stack.38.scal_ref, f32[32,2]{1,0:T(8,128)} %broadcast_subtract_fusion.dtab_ref, bf16[1024,128]{1,0:T(8,128)(2,1)} %pad_maximum_fusion.1.q_ref, bf16[16384,256]{1,0:T(8,128)(2,1)} %all-gather.5.cloned.1.call-done.k_ref.v_ref, ...), custom_call_target="tpu_custom_call" | custom-call | flops 34359738368 | bytes 11534336 | tf_op jit(solution)/shard_map/pallas_call | solution.py:128
  230.4 1.6 fusion.21
  232.0 2.6 collective-permute-start.1
  234.6 6.3 %collective-permute-done.1 = bf16[512,128]{1,0:T(8,128)(2,1)S(1)} collective-permute-done((bf16[512,128]{1,0:T(8,128)(2,1)S(1)}, bf16[512,128]{1,0:T(8,128)(2,1)S(1)}, u32[]{:S(2)}, u32[]{:S(2)}) %collective-permute-start.1) | collective-permute-done | bytes 131104 | tf_op jit(solution)/shard_map/ppermute | solution.py:233
  240.9 0.7 pad_maximum_fusion.2
  242.0 0.3 eq.26
  242.2 0.3 reshape.92
  242.5 2.6 copy.41
  245.1 2.3 reduce-window.6
  247.4 0.3 slice_reduce_fusion
  247.8 0.2 copy.47
  248.1 0.3 mul.107
  248.5 0.5 reduce_sum.32
  249.1 8.1 %scatter_custom_fusion = s32[3072]{0:T(1024)S(1)} fusion(s32[2048]{0:T(1024)S(1)} %bitcast.66, s32[2048]{0:T(1024)S(1)} %add_select_fusion, s32[]{:T(128)} %constant.47.clone.1), kind=kCustom, calls=%fused_computation.59 | custom fusion | bytes 12292 | tf_op jit(solution)/shard_map/scatter | solution.py:252
  257.4 0.3 copy.46
  258.0 31.7 %all-gather.9.cloned.1.call-done = bf16[1024,1024]{1,0:T(8,128)(2,1)} async-done(((bf16[1024,128]{1,0:T(8,128)(2,1)}), bf16[1024,1024]{1,0:T(8,128)(2,1)}) %all-gather.9.cloned.1.call-update) | async-done | bytes 2097168 | tf_op jit(solution)/shard_map/all_gather | solution.py:234
  289.7 5.4 %multiply_reduce_fusion.1 = (f32[1024]{0:T(1024)S(1)}, f32[1024,1024]{0,1:T(8,128)S(1)}) fusion(bf16[1024,1024]{1,0:T(8,128)(2,1)} %all-gather.9.cloned.1.call-done, bf16[1024,1024]{1,0:T(8,128)(2,1)} %all-gather.11.cloned.1.call-done, bf16[1024,1024]{0,1:T(8,128)(2,1)} %copy.41), kind=kOutput, calls=%fused_computation.21 | convolution fusion | flops 2151676928 | bytes 10489856 | tf_op jit(solution)/shard_map/dot_general | solution.py:238
  295.1 2.0 copy-done
  297.1 1.7 multiply_convert_fusion
  298.8 3.0 copy.48
  301.9 14.0 %gather_fusion = bf16[3072,1024]{1,0:T(8,128)(2,1)} fusion(bf16[1024,1024]{1,0:T(8,128)(2,1)S(1)} %copy.48, s32[3072]{0:T(1024)S(1)} %fusion.26), kind=kCustom, calls=%fused_computation | custom fusion | bytes 12595200 | tf_op jit(solution)/shard_map/jit(_take)/gather | solution.py:253
  315.9 15.6 %fusion = f32[8,384,2,352]{1,3,2,0:T(8,128)} fusion(bf16[8,1024,2,352]{1,3,2,0:T(8,128)(2,1)} %param.26, bf16[8,384,1024]{2,1,0:T(8,128)(2,1)} %bitcast.64, pred[8,384]{1,0:T(8,128)(4,1)S(1)} %broadcast_in_dim.55), kind=kOutput, calls=%fused_computation.5 | convolution fusion | flops 4432330752 | bytes 26479616 | tf_op jit(solution)/shard_map/ecd,edgf->ecgf/dot_general | solution.py:254
  331.4 13.3 %fusion.14 = f32[8,384,1024]{2,1,0:T(8,128)} fusion(bf16[8,352,1024]{2,1,0:T(8,128)(2,1)} %param.27, f32[8,384,2,352]{1,3,2,0:T(8,128)} %fusion), kind=kOutput, calls=%fused_computation.24 | convolution fusion | flops 2225405952 | bytes 27000832 | tf_op jit(solution)/shard_map/ecf,efd->ecd/dot_general | solution.py:258
  344.7 16.3 %gather_fusion.1 = f32[2048,1024]{1,0:T(8,128)} fusion(f32[3072,1024]{1,0:T(8,128)} %bitcast.63, s32[2048]{0:T(1024)S(1)} %broadcast_clamp_fusion), kind=kCustom, calls=%fused_computation.1 | custom fusion | bytes 16785408 | tf_op jit(solution)/shard_map/jit(_take)/gather | solution.py:261
  361.0 10.6 %gather.15 = f32[1024,2,1024]{2,1,0:T(2,128)} reshape(f32[2048,1024]{1,0:T(8,128)} %gather_fusion.1) | data formatting | bytes 16777216 | tf_op jit(solution)/shard_map/jit(_take)/gather | solution.py:261
  371.6 17.6 %multiply_reduce_fusion = bf16[1024,1024]{1,0:T(8,128)(2,1)S(1)} fusion(f32[1024,2,1024]{2,1,0:T(2,128)} %gather.15, pred[1024,2]{1,0:T(8,128)(4,1)S(1)} %copy.46, f32[1024,2]{1,0:T(8,128)S(1)} %copy.50), kind=kLoop, calls=%fused_computation.3 | loop fusion | flops 5242880 | bytes 10496000 | tf_op jit(solution)/shard_map/reduce_sum | solution.py:262
  389.2 2.6 copy.51
  391.7 56.2 %reduce-scatter.2.cloned.1.call-done = bf16[1024,128]{0,1:T(8,128)(2,1)} async-done(((bf16[1024,1024]{0,1:T(8,128)(2,1)}), bf16[1024,128]{0,1:T(8,128)(2,1)}) %reduce-scatter.2.cloned.1.call-update) | async-done | bytes 262160 | tf_op jit(solution)/shard_map/reduce_scatter | solution.py:263
  447.9 1.2 add_convert_fusion
  449.1 0.8 copy.52
  (42 shorter events, 1.3 us)
Async XLA Ops:
  6.5 70.8 %all-gather.7.cloned.1.call-start = ((), (), s32[]{:S(2)}) async-start(), calls=%async_computation.2 | async-start | bytes 6684672 | tf_op jit(solution)/shard_map/all_gather | solution.py:207
  8.4 151.3 %all-gather.5.cloned.1.call-start = ((), (), s32[]{:S(2)}) async-start(), calls=%async_computation.1 | async-start | bytes 8912896 | tf_op jit(solution)/shard_map/all_gather | solution.py:219
  10.5 0.8 copy-start.2
  11.3 246.7 %all-gather.11.cloned.1.call-start = ((), (), s32[]{:S(2)}) async-start(), calls=%async_computation.4 | async-start | bytes 2359296 | tf_op jit(solution)/shard_map/all_gather | solution.py:235
  12.3 11.9 %collective-permute-start = (bf16[512,128]{1,0:T(8,128)(2,1)S(1)}, bf16[512,128]{1,0:T(8,128)(2,1)S(1)}, u32[]{:S(2)}, u32[]{:S(2)}) collective-permute-start(bf16[512,128]{1,0:T(8,128)(2,1)S(1)} %get-tuple-element.24), channel_id=1, source_target_pairs={{0,120},{8,112},{16,104},{24,96},{32,88},{40,80},{48,72},{56,64},{... | collective-permute-start | bytes 393224 | tf_op jit(solution)/shard_map/ppermute | solution.py:188
  20.0 269.6 %all-gather.9.cloned.1.call-start = ((), (), s32[]{:S(2)}) async-start(), calls=%async_computation.3 | async-start | bytes 2359296 | tf_op jit(solution)/shard_map/all_gather | solution.py:234
  159.7 82.0 %copy-start.3 = (s32[1024,2]{0,1:T(2,128)S(1)}, s32[1024,2]{0,1:T(2,128)}, u32[]{:S(2)}) copy-start(s32[1024,2]{0,1:T(2,128)} %param.24) | copy-start | bytes 24580
  230.4 12.1 %copy-start.1 = (bf16[1024,1024]{1,0:T(8,128)(2,1)S(1)}, bf16[1024,1024]{1,0:T(8,128)(2,1)}, u32[]{:S(2)}) copy-start(bf16[1024,1024]{1,0:T(8,128)(2,1)} %param.14) | copy-start | bytes 6291460
  232.0 8.9 %collective-permute-start.1 = (bf16[512,128]{1,0:T(8,128)(2,1)S(1)}, bf16[512,128]{1,0:T(8,128)(2,1)S(1)}, u32[]{:S(2)}, u32[]{:S(2)}) collective-permute-start(bf16[512,128]{1,0:T(8,128)(2,1)S(1)} %get-tuple-element.22), channel_id=1, source_target_pairs={{0,120},{8,112},{16,104},{24,96},{32,88},{40,80},{48,72},{56,64},{... | collective-permute-start | bytes 393224 | tf_op jit(solution)/shard_map/ppermute | solution.py:233
  241.7 16.0 %copy-start.4 = (f32[1024,2]{0,1:T(2,128)S(1)}, f32[1024,2]{0,1:T(2,128)}, u32[]{:S(2)}) copy-start(f32[1024,2]{0,1:T(2,128)} %param.25) | copy-start | bytes 24580
  241.7 206.3 %reduce-scatter.2.cloned.1.call-start = ((), (), s32[]{:S(2)}) async-start(), calls=%async_computation.5 | async-start | bytes 2359296 | tf_op jit(solution)/shard_map/reduce_scatter | solution.py:263
  257.9 39.2 %copy-start.5 = (f32[1024]{0:T(1024)S(1)}, f32[1024]{0:T(1024)}, u32[]{:S(2)}) copy-start(f32[1024]{0:T(1024)} %param.23) | copy-start | bytes 12292
  295.1 2.0 copy-start
Sparse Core Ops, SparseCore 0:
  9.8 67.4 all-gather.6
  79.8 70.5 all-gather.4
  152.1 48.6 all-gather.10
  241.8 47.8 all-gather.8
  391.9 56.0 reduce-scatter.1

commit v6 on v5

--- a/solution.py
+++ b/solution.py
@@ -12,7 +12,7 @@
 TOP = 2
 CAP = 384
 KEY_TILE = 512
-ROW_BLOCK = 256
+ROW_BLOCK = 512
 
 
 bucket_edges = [edge for edge in range(1, 17)] + [

time: 466 us -> 448 us (0.961)
  Pallas kernels: 169 us -> 138 us
  waiting for transfers between devices: 127 us -> 141 us
    pallas_call x3, Pallas kernels: 169 us -> 138 us  [attend(): pl.pallas_call(attn_kernel, out_shape=(jax.ShapeDtypeStruct(m.shape, jnp....]
    all_gather x1, waiting for transfers between devices: 0.01 us -> 13.2 us  [per_device(): all_pairs = lax.all_gather(own_pairs, 'seq', axis=0, tiled=True)]
  transfers between devices with their start and end apart: 7 -> 7, of which waited for: 4 -> 5; matrix products, arithmetic and copies ran while one was open for 6% -> 7% of each run, Pallas kernels for 37% -> 32%
where the time goes in v6:
time: 448 us; the launch traced here: 439 us
  waiting for transfers between devices  141 us (31%)
  Pallas kernels  138 us (31%)
  local copies, waits for them, and re-layouts  71.7 us (16%)
  matrix products  34.3 us (8%)
  other arithmetic  29.2 us (7%)
  between operations  14.3 us (3%)
  starting transfers between devices  9.78 us (2%)
    pallas_call x3, Pallas kernels, attend(): pl.pallas_call(attn_kernel, out_shape=(jax.ShapeDtypeStruct(m.shape, jnp....  138 us
    reduce_scatter x1, waiting for transfers between devices, per_device(): lax.psum_scatter(combined.astype(jnp.bfloat16), 'tensor', scatter_dimensi...  56.9 us
    all_gather x1, waiting for transfers between devices, per_device(): lax.all_gather(jnp.concatenate([cached_keys, cached_values], 1), 'seq', a...  34.4 us
    all_gather x1, waiting for transfers between devices, per_device(): attended_full = lax.all_gather(attended, 'tensor', axis=1, tiled=True)  30.5 us
    gather x2, local copies, waits for them, and re-layouts, per_device(): picked = jnp.take(expert_rows, target, axis=0).reshape(tok_rows, TOP, D)  26.8 us
    reduce_sum x1, other arithmetic, per_device(): combined = jnp.sum(picked * route_weights[:, :, None], axis=1)  17.5 us
    dot_general x1, matrix products, per_device(): jnp.einsum('ecd,edgf->ecgf', buffer, expert_in, preferred_element_type=jn...  15.6 us
    gather x1, local copies, waits for them, and re-layouts, per_device(): buffer = jnp.take(normed, slot_owner, axis=0).reshape(expert_count, CAP, D)  14 us
  transfers between devices with their start and end apart: 7, of which 5 were waited for; matrix products, arithmetic and copies ran while one was open for 7% of the time, Pallas kernels for 32%

profile of v6, /device:TPU:1, one launch (start us, length us, event | category | flops | bytes accessed | tf_op | source)
XLA Modules:
  0.0 439.1 jit_solution(4901994980746919055)
XLA Ops:
  6.5 1.8 pad_maximum_fusion
  8.4 1.0 constant_dynamic-update-slice_fusion.1
  9.4 1.0 constant_dynamic-update-slice_fusion.k_ref.v_ref
  10.5 0.8 copy-done.2
  11.3 1.0 fusion.38
  12.3 7.7 %collective-permute-start = (bf16[512,128]{1,0:T(8,128)(2,1)S(1)}, bf16[512,128]{1,0:T(8,128)(2,1)S(1)}, u32[]{:S(2)}, u32[]{:S(2)}) collective-permute-start(bf16[512,128]{1,0:T(8,128)(2,1)S(1)} %get-tuple-element.24), channel_id=1, source_target_pairs={{0,120},{8,112},{16,104},{24,96},{32,88},{40,80},{48,72},{56,64},{... | collective-permute-start | bytes 393224 | tf_op jit(solution)/shard_map/ppermute | solution.py:188
  20.1 0.8 copy.42
  20.8 0.9 slice_reduce_fusion.1
  21.7 0.6 broadcast_subtract_fusion.dtab_ref
  23.0 0.7 stack.38.scal_ref
  23.6 0.6 pad_add_fusion
  24.3 0.7 pad_maximum_fusion.1.q_ref
  25.0 1.0 broadcast_in_dim.49.m_in
  26.0 1.1 broadcast_in_dim.50.l_in
  27.1 0.8 broadcast_in_dim.51.acc_in
  27.9 14.9 %shard_map.136 = (f32[2,1024,128]{2,1,0:T(8,128)}, f32[2,1024,128]{2,1,0:T(8,128)}, f32[1024,128]{1,0:T(8,128)}) custom-call(s32[5]{0:T(128)} %get-tuple-element.25.scal_ref, f32[32,2]{1,0:T(8,128)} %broadcast_subtract_fusion.dtab_ref, bf16[1024,128]{1,0:T(8,128)(2,1)} %pad_maximum_fusion.1.q_ref, bf16[1024,256]{1,0:T(8,128)(2,1)} %copy-done.2, ...), custom_call_target="tpu_custom_call" | custom-call | flops 2147483648 | bytes 3670016 | tf_op jit(solution)/shard_map/pallas_call | solution.py:128
  42.9 34.4 %all-gather.7.cloned.1.call-done.k_ref.v_ref = bf16[12288,256]{1,0:T(8,128)(2,1)} async-done(((bf16[768,256]{1,0:T(8,128)(2,1)}), bf16[12288,256]{1,0:T(8,128)(2,1)}) %all-gather.7.cloned.1.call-update) | async-done | bytes 6291472 | tf_op jit(solution)/shard_map/all_gather | solution.py:207
  77.3 59.8 %shard_map.137 = (f32[2,1024,128]{2,1,0:T(8,128)}, f32[2,1024,128]{2,1,0:T(8,128)}, f32[1024,128]{1,0:T(8,128)}) custom-call(s32[5]{0:T(128)} %get-tuple-element.26.scal_ref, f32[32,2]{1,0:T(8,128)} %broadcast_subtract_fusion.dtab_ref, bf16[1024,128]{1,0:T(8,128)(2,1)} %pad_maximum_fusion.1.q_ref, ...), custom_call_target="tpu_custom_call" | custom-call | flops 25769803776 | bytes 9437184 | tf_op jit(solution)/shard_map/pallas_call | solution.py:128
  137.2 13.2 %all-gather.5.cloned.1.call-done.k_ref.v_ref = bf16[16384,256]{1,0:T(8,128)(2,1)} async-done(((bf16[1024,256]{1,0:T(8,128)(2,1)}), bf16[16384,256]{1,0:T(8,128)(2,1)}) %all-gather.5.cloned.1.call-update) | async-done | bytes 8388624 | tf_op jit(solution)/shard_map/all_gather | solution.py:219
  150.4 63.7 %shard_map.138 = (f32[2,1024,128]{2,1,0:T(8,128)}, f32[2,1024,128]{2,1,0:T(8,128)}, f32[1024,128]{1,0:T(8,128)}) custom-call(s32[5]{0:T(128)} %stack.38.scal_ref, f32[32,2]{1,0:T(8,128)} %broadcast_subtract_fusion.dtab_ref, bf16[1024,128]{1,0:T(8,128)(2,1)} %pad_maximum_fusion.1.q_ref, bf16[16384,256]{1,0:T(8,128)(2,1)} %all-gather.5.cloned.1.call-done.k_ref.v_ref, ...), custom_call_target="tpu_custom_call" | custom-call | flops 34359738368 | bytes 11534336 | tf_op jit(solution)/shard_map/pallas_call | solution.py:128
  214.0 1.6 fusion.21
  215.7 1.9 collective-permute-start.1
  217.6 6.2 %collective-permute-done.1 = bf16[512,128]{1,0:T(8,128)(2,1)S(1)} collective-permute-done((bf16[512,128]{1,0:T(8,128)(2,1)S(1)}, bf16[512,128]{1,0:T(8,128)(2,1)S(1)}, u32[]{:S(2)}, u32[]{:S(2)}) %collective-permute-start.1) | collective-permute-done | bytes 131104 | tf_op jit(solution)/shard_map/ppermute | solution.py:233
  223.8 0.7 pad_maximum_fusion.2
  224.8 0.3 eq.26
  225.1 0.3 reshape.92
  225.3 2.7 copy.41
  228.1 2.3 reduce-window.6
  230.4 0.3 slice_reduce_fusion
  231.1 0.3 mul.107
  231.5 0.5 reduce_sum.32
  232.0 8.1 %scatter_custom_fusion = s32[3072]{0:T(1024)S(1)} fusion(s32[2048]{0:T(1024)S(1)} %bitcast.66, s32[2048]{0:T(1024)S(1)} %add_select_fusion, s32[]{:T(128)} %constant.47.clone.1), kind=kCustom, calls=%fused_computation.59 | custom fusion | bytes 12292 | tf_op jit(solution)/shard_map/scatter | solution.py:252
  240.4 0.3 copy.46
  241.0 30.5 %all-gather.9.cloned.1.call-done = bf16[1024,1024]{1,0:T(8,128)(2,1)} async-done(((bf16[1024,128]{1,0:T(8,128)(2,1)}), bf16[1024,1024]{1,0:T(8,128)(2,1)}) %all-gather.9.cloned.1.call-update) | async-done | bytes 2097168 | tf_op jit(solution)/shard_map/all_gather | solution.py:234
  271.5 5.4 %multiply_reduce_fusion.1 = (f32[1024]{0:T(1024)S(1)}, f32[1024,1024]{0,1:T(8,128)S(1)}) fusion(bf16[1024,1024]{1,0:T(8,128)(2,1)} %all-gather.9.cloned.1.call-done, bf16[1024,1024]{1,0:T(8,128)(2,1)} %all-gather.11.cloned.1.call-done, bf16[1024,1024]{0,1:T(8,128)(2,1)} %copy.41), kind=kOutput, calls=%fused_computation.21 | convolution fusion | flops 2151676928 | bytes 10489856 | tf_op jit(solution)/shard_map/dot_general | solution.py:238
  277.0 2.0 copy-done
  279.0 1.7 multiply_convert_fusion
  280.7 2.9 copy.48
  283.6 14.0 %gather_fusion = bf16[3072,1024]{1,0:T(8,128)(2,1)} fusion(bf16[1024,1024]{1,0:T(8,128)(2,1)S(1)} %copy.48, s32[3072]{0:T(1024)S(1)} %fusion.26), kind=kCustom, calls=%fused_computation | custom fusion | bytes 12595200 | tf_op jit(solution)/shard_map/jit(_take)/gather | solution.py:253
  297.5 15.6 %fusion = f32[8,384,2,352]{1,3,2,0:T(8,128)} fusion(bf16[8,1024,2,352]{1,3,2,0:T(8,128)(2,1)} %param.26, bf16[8,384,1024]{2,1,0:T(8,128)(2,1)} %bitcast.64, pred[8,384]{1,0:T(8,128)(4,1)S(1)} %broadcast_in_dim.55), kind=kOutput, calls=%fused_computation.5 | convolution fusion | flops 4432330752 | bytes 26479616 | tf_op jit(solution)/shard_map/ecd,edgf->ecgf/dot_general | solution.py:254
  313.1 13.3 %fusion.14 = f32[8,384,1024]{2,1,0:T(8,128)} fusion(bf16[8,352,1024]{2,1,0:T(8,128)(2,1)} %param.27, f32[8,384,2,352]{1,3,2,0:T(8,128)} %fusion), kind=kOutput, calls=%fused_computation.24 | convolution fusion | flops 2225405952 | bytes 27000832 | tf_op jit(solution)/shard_map/ecf,efd->ecd/dot_general | solution.py:258
  326.4 16.3 %gather_fusion.1 = f32[2048,1024]{1,0:T(8,128)} fusion(f32[3072,1024]{1,0:T(8,128)} %bitcast.63, s32[2048]{0:T(1024)S(1)} %broadcast_clamp_fusion), kind=kCustom, calls=%fused_computation.1 | custom fusion | bytes 16785408 | tf_op jit(solution)/shard_map/jit(_take)/gather | solution.py:261
  342.7 10.6 %gather.15 = f32[1024,2,1024]{2,1,0:T(2,128)} reshape(f32[2048,1024]{1,0:T(8,128)} %gather_fusion.1) | data formatting | bytes 16777216 | tf_op jit(solution)/shard_map/jit(_take)/gather | solution.py:261
  353.2 17.5 %multiply_reduce_fusion = bf16[1024,1024]{1,0:T(8,128)(2,1)S(1)} fusion(f32[1024,2,1024]{2,1,0:T(2,128)} %gather.15, pred[1024,2]{1,0:T(8,128)(4,1)S(1)} %copy.46, f32[1024,2]{1,0:T(8,128)S(1)} %copy.50), kind=kLoop, calls=%fused_computation.3 | loop fusion | flops 5242880 | bytes 10496000 | tf_op jit(solution)/shard_map/reduce_sum | solution.py:262
  370.8 2.6 copy.51
  373.4 56.9 %reduce-scatter.2.cloned.1.call-done = bf16[1024,128]{0,1:T(8,128)(2,1)} async-done(((bf16[1024,1024]{0,1:T(8,128)(2,1)}), bf16[1024,128]{0,1:T(8,128)(2,1)}) %reduce-scatter.2.cloned.1.call-update) | async-done | bytes 262160 | tf_op jit(solution)/shard_map/reduce_scatter | solution.py:263
  430.3 1.2 add_convert_fusion
  431.5 0.8 copy.52
  (42 shorter events, 1.6 us)
Async XLA Ops:
  6.5 70.8 %all-gather.7.cloned.1.call-start = ((), (), s32[]{:S(2)}) async-start(), calls=%async_computation.2 | async-start | bytes 6684672 | tf_op jit(solution)/shard_map/all_gather | solution.py:207
  8.4 142.0 %all-gather.5.cloned.1.call-start = ((), (), s32[]{:S(2)}) async-start(), calls=%async_computation.1 | async-start | bytes 8912896 | tf_op jit(solution)/shard_map/all_gather | solution.py:219
  10.5 0.8 copy-start.2
  11.3 229.7 %all-gather.11.cloned.1.call-start = ((), (), s32[]{:S(2)}) async-start(), calls=%async_computation.4 | async-start | bytes 2359296 | tf_op jit(solution)/shard_map/all_gather | solution.py:235
  12.3 11.9 %collective-permute-start = (bf16[512,128]{1,0:T(8,128)(2,1)S(1)}, bf16[512,128]{1,0:T(8,128)(2,1)S(1)}, u32[]{:S(2)}, u32[]{:S(2)}) collective-permute-start(bf16[512,128]{1,0:T(8,128)(2,1)S(1)} %get-tuple-element.24), channel_id=1, source_target_pairs={{0,120},{8,112},{16,104},{24,96},{32,88},{40,80},{48,72},{56,64},{... | collective-permute-start | bytes 393224 | tf_op jit(solution)/shard_map/ppermute | solution.py:188
  20.0 251.5 %all-gather.9.cloned.1.call-start = ((), (), s32[]{:S(2)}) async-start(), calls=%async_computation.3 | async-start | bytes 2359296 | tf_op jit(solution)/shard_map/all_gather | solution.py:234
  150.4 74.2 %copy-start.3 = (s32[1024,2]{0,1:T(2,128)S(1)}, s32[1024,2]{0,1:T(2,128)}, u32[]{:S(2)}) copy-start(s32[1024,2]{0,1:T(2,128)} %param.24) | copy-start | bytes 24580
  214.0 11.3 %copy-start.1 = (bf16[1024,1024]{1,0:T(8,128)(2,1)S(1)}, bf16[1024,1024]{1,0:T(8,128)(2,1)}, u32[]{:S(2)}) copy-start(bf16[1024,1024]{1,0:T(8,128)(2,1)} %param.14) | copy-start | bytes 6291460
  215.7 8.1 %collective-permute-start.1 = (bf16[512,128]{1,0:T(8,128)(2,1)S(1)}, bf16[512,128]{1,0:T(8,128)(2,1)S(1)}, u32[]{:S(2)}, u32[]{:S(2)}) collective-permute-start(bf16[512,128]{1,0:T(8,128)(2,1)S(1)} %get-tuple-element.22), channel_id=1, source_target_pairs={{0,120},{8,112},{16,104},{24,96},{32,88},{40,80},{48,72},{56,64},{... | collective-permute-start | bytes 393224 | tf_op jit(solution)/shard_map/ppermute | solution.py:233
  224.5 16.2 %copy-start.4 = (f32[1024,2]{0,1:T(2,128)S(1)}, f32[1024,2]{0,1:T(2,128)}, u32[]{:S(2)}) copy-start(f32[1024,2]{0,1:T(2,128)} %param.25) | copy-start | bytes 24580
  224.5 205.8 %reduce-scatter.2.cloned.1.call-start = ((), (), s32[]{:S(2)}) async-start(), calls=%async_computation.5 | async-start | bytes 2359296 | tf_op jit(solution)/shard_map/reduce_scatter | solution.py:263
  240.9 38.0 %copy-start.5 = (f32[1024]{0:T(1024)S(1)}, f32[1024]{0:T(1024)}, u32[]{:S(2)}) copy-start(f32[1024]{0:T(1024)} %param.23) | copy-start | bytes 12292
  277.0 2.0 copy-start
Sparse Core Ops, SparseCore 0:
  9.8 67.4 all-gather.6
  79.8 70.5 all-gather.4
  152.0 48.7 all-gather.10
  224.6 46.8 all-gather.8
  373.5 56.7 reduce-scatter.1
